TPU v7x, 32 devices: a whole 2x2x4 slice. The times are simulated.
32 devices in a mesh: bond: 4 (over x, core), rows: 8 (over z, y).
Axes of the slice: x: 2, y: 2, z: 4, core: 2. Of those that a mesh axis runs over, the one named last changes fastest.
Arguments:
- amps_left: float32 [2, 4096, 12288], P(None, 'rows', 'bond'), may hold values from -0.0390625 to 0.0390625
- amps_right: float32 [2, 512, 12288], P(None, 'rows', 'bond'), may hold values from -6 to 6
- axis_order: int32 [21], replicated, may hold values from 0 to 20, as said below
Outputs:
- regrouped: float32 [2, 4096, 512], P(None, 'rows', 'bond')
Inputs may be any that keep to these rules, and one draw needn't show every extreme that they name: axis_order is a permutation. For every bit p of the result among its highest log2 * 8 row bits and its highest log2 * 4 column bits, axis_order[p] is none of: the highest log2 * 8 row bits of the product, the log2 * 4 row bits just below them, the highest log2 * 4 column bits of the product. Bits count from the least significant bit of the flat index, columns first.
All inputs are finite; a program needn't handle non-finite values.
Results may differ from a plain program's by a relative error of at most 0.00007.
Values sent between devices are 32-bit elements; how exact they have to be, the bound alone decides.
No kernel may reach another device: no remote copies, remote signals or barrier semaphores. Data moves between devices by JAX's collectives and lax.ppermute only.
A program may use at most 128 MiB of HBM per device.

v0:
```python
import jax
import jax.numpy as jnp
from jax import lax
from jax.sharding import PartitionSpec as P

ROW_BITS = 12
COL_BITS = 9


def cross_dot(left, right):
    return lax.dot_general(
        left,
        right,
        (((1,), (1,)), ((), ())),
        precision=lax.Precision.HIGH,
        preferred_element_type=jnp.float32,
    )


def rank_within(keys, member):
    below = (keys[None, :] < keys[:, None]) & member[None, :]
    return jnp.sum(below.astype(jnp.int32), axis=1)


def perm_matrix(new_pos, nbits):
    old = jnp.arange(2**nbits, dtype=jnp.int32)
    moved = jnp.zeros_like(old)
    for bit_num in range(nbits):
        moved = moved + jnp.left_shift(jnp.right_shift(old, bit_num) & 1, new_pos[bit_num])
    return (old[:, None] == moved[None, :]).astype(jnp.float32)


def permute_rows(block, mat):
    return jnp.einsum("no,pol->pnl", mat, block, precision=lax.Precision.HIGHEST)


def permute_lanes(block, mat):
    return jnp.einsum("no,pro->prn", mat, block, precision=lax.Precision.HIGHEST)


def cross_swap(block, m, rbits, cbits):
    def branch(k):
        def run(x):
            planes = x.shape[0]
            x = x.reshape(planes, 2 ** (rbits - k), 2**k, 2**k, 2 ** (cbits - k))
            x = jnp.transpose(x, (0, 1, 3, 2, 4))
            return x.reshape(planes, 2**rbits, 2**cbits)

        return run

    return lax.switch(m, [branch(k) for k in range(min(rbits, cbits) + 1)], block)


def plan_permute(src, rbits, cbits):
    total = rbits + cbits
    dest_of = jnp.zeros((total,), jnp.int32).at[src].set(jnp.arange(total, dtype=jnp.int32))
    pos = jnp.arange(total, dtype=jnp.int32)
    is_lane = pos < cbits
    goes_lane = dest_of < cbits
    lane_stay = is_lane & goes_lane
    lane_go = is_lane & ~goes_lane
    row_stay = ~is_lane & ~goes_lane
    row_go = ~is_lane & goes_lane
    m = jnp.sum(row_go.astype(jnp.int32))
    r_lane_stay = rank_within(dest_of, lane_stay)
    r_lane_go = rank_within(dest_of, lane_go)
    r_row_stay = rank_within(dest_of, row_stay)
    r_row_go = rank_within(dest_of, row_go)
    first_rows = jnp.where(row_go, r_row_go, m + r_row_stay)[cbits:]
    first_lanes = jnp.where(lane_go, cbits - m + r_lane_go, r_lane_stay)[:cbits]
    lane_src_pos = jnp.where(lane_stay, r_lane_stay, cbits - m + r_row_go)
    lane_members = lane_stay | row_go
    row_src_pos = jnp.where(lane_go, r_lane_go, m + r_row_stay)
    row_members = lane_go | row_stay
    second_lanes = jnp.zeros((cbits,), jnp.int32).at[
        jnp.where(lane_members, lane_src_pos, cbits)
    ].set(dest_of, mode="drop")
    second_rows = jnp.zeros((rbits,), jnp.int32).at[
        jnp.where(row_members, row_src_pos, rbits)
    ].set(dest_of - cbits, mode="drop")
    mats = (
        perm_matrix(first_rows, rbits),
        perm_matrix(first_lanes, cbits),
        perm_matrix(second_rows, rbits),
        perm_matrix(second_lanes, cbits),
    )
    return mats, m


def apply_permute(block, plan):
    (rows_a, lanes_a, rows_b, lanes_b), m = plan
    rbits = block.shape[1].bit_length() - 1
    cbits = block.shape[2].bit_length() - 1
    block = permute_rows(block, rows_a)
    block = permute_lanes(block, lanes_a)
    block = cross_swap(block, m, rbits, cbits)
    block = permute_rows(block, rows_b)
    return permute_lanes(block, lanes_b)


def make_plans(axis_order):
    nrows = lax.axis_size("rows")
    nbond = lax.axis_size("bond")
    row_devbits = nrows.bit_length() - 1
    bond_devbits = nbond.bit_length() - 1
    total_bits = ROW_BITS + COL_BITS
    lrows = ROW_BITS - row_devbits
    lcols = COL_BITS - bond_devbits
    nlocal = lrows + lcols
    devbits = row_devbits + bond_devbits
    local_of = []
    for bit in range(total_bits):
        if bit < lcols:
            local_of.append(bit)
        elif COL_BITS <= bit < COL_BITS + lrows:
            local_of.append(bit - COL_BITS + lcols)
        else:
            local_of.append(-1)
    local_of = jnp.array(local_of, dtype=jnp.int32)
    out_dev = [COL_BITS + lrows + k for k in range(row_devbits)] + [
        lcols + k for k in range(bond_devbits)
    ]
    dev_src = local_of[axis_order[jnp.array(out_dev, dtype=jnp.int32)]]
    pos = jnp.arange(nlocal, dtype=jnp.int32)
    is_dev = jnp.any(pos[:, None] == dev_src[None, :], axis=1)
    keep = ~is_dev
    keep_rank = rank_within(pos, keep)
    src_a = jnp.zeros((nlocal,), jnp.int32).at[
        jnp.where(keep, keep_rank, nlocal)
    ].set(pos, mode="drop")
    src_a = src_a.at[nlocal - devbits + jnp.arange(devbits)].set(dev_src)
    plan_a = plan_permute(src_a, lrows, lcols)
    src_dev_bits = [COL_BITS + lrows + k for k in range(row_devbits)] + [
        lcols + k for k in range(bond_devbits)
    ]
    pos_w = jnp.full((total_bits,), -1, jnp.int32)
    within = jnp.zeros((nlocal,), jnp.int32).at[jnp.where(keep, keep_rank, nlocal)].set(
        pos, mode="drop"
    )
    prod_of_local = jnp.array(
        [b for b in range(total_bits) if b < lcols]
        + [b for b in range(COL_BITS, COL_BITS + lrows)],
        dtype=jnp.int32,
    )
    pos_w = pos_w.at[prod_of_local[within[: nlocal - devbits]]].set(
        jnp.arange(nlocal - devbits, dtype=jnp.int32)
    )
    pos_w = pos_w.at[jnp.array(src_dev_bits, dtype=jnp.int32)].set(
        nlocal - devbits + jnp.arange(devbits, dtype=jnp.int32)
    )
    out_local = [b for b in range(lcols)] + [COL_BITS + k for k in range(lrows)]
    src_c = pos_w[axis_order[jnp.array(out_local, dtype=jnp.int32)]]
    plan_c = plan_permute(src_c, lrows, lcols)
    return plan_a, plan_c


def regroup(block, plans):
    plan_a, plan_c = plans
    planes, nrow, ncol = block.shape
    devices = lax.axis_size("rows") * lax.axis_size("bond")
    block = apply_permute(block, plan_a)
    block = block.reshape(planes, devices, -1)
    block = lax.all_to_all(block, ("bond", "rows"), split_axis=1, concat_axis=1, tiled=True)
    block = block.reshape(planes, nrow, ncol)
    return apply_permute(block, plan_c)


def ring_all_gather(shard, axis):
    size = lax.axis_size(axis)
    ring = [2 * k for k in range(size // 2)] + [2 * k + 1 for k in reversed(range(size // 2))]
    pos_of = [ring.index(idx) for idx in range(size)]
    fwd = [(ring[i], ring[(i + 1) % size]) for i in range(size)]
    bwd = [(ring[(i + 1) % size], ring[i]) for i in range(size)]
    me = lax.axis_index(axis)
    my_pos = jnp.array(pos_of, dtype=jnp.int32)[me]
    ring_arr = jnp.array(ring, dtype=jnp.int32)
    planes, rows, width = shard.shape
    half = rows // 2
    ahead, behind = shard[:, :half], shard[:, half:]
    zero = jnp.int32(0)
    out = jnp.zeros((planes, size * rows, width), shard.dtype)
    out = lax.dynamic_update_slice(out, shard, (zero, me * rows, zero))
    for step in range(1, size):
        ahead = lax.ppermute(ahead, axis, fwd)
        behind = lax.ppermute(behind, axis, bwd)
        src_ahead = ring_arr[(my_pos - step) % size]
        src_behind = ring_arr[(my_pos + step) % size]
        out = lax.dynamic_update_slice(out, ahead, (zero, src_ahead * rows, zero))
        out = lax.dynamic_update_slice(out, behind, (zero, src_behind * rows + half, zero))
    return out


def per_device(amps_left, amps_right, axis_order):
    plans = make_plans(axis_order)
    gathered = ring_all_gather(amps_right, "rows")
    gathered, plans = lax.optimization_barrier((gathered, plans))
    real_part = cross_dot(amps_left[0], gathered[0]) - cross_dot(amps_left[1], gathered[1])
    imag_part = cross_dot(amps_left[0], gathered[1]) + cross_dot(amps_left[1], gathered[0])
    partial_sums = jnp.stack([real_part, imag_part])
    block = lax.psum_scatter(partial_sums, "bond", scatter_dimension=2, tiled=True)
    return regroup(block, plans)


def solution(mesh):
    placed = (P(None, "rows", "bond"), P(None, "rows", "bond"), P())
    return jax.shard_map(
        per_device, mesh=mesh, in_specs=placed, out_specs=P(None, "rows", "bond"), check_vma=False
    )
```

profile of v0, /device:TPU:0, one launch (start us, length us, event | category | flops | bytes accessed | tf_op | source)
XLA Modules:
  0.0 314.5 jit_solution(7357476552149331494)
XLA Ops:
  31.5 4.3 %shift-left_add_fusion.4 = s32[128]{0:T(128)S(1)} fusion(s32[]{:T(128)} %bitcast.127, s32[]{:T(128)} %bitcast.126, s32[]{:T(128)} %bitcast.125, s32[]{:T(128)} %bitcast.124, s32[]{:T(128)} %bitcast.123, s32[]{:T(128)} %bitcast.122, s32[]{:T(128)} %bitcast.121), kind=kLoop, calls=%fused_computation.154 | loop fusion | flops 3456 | bytes 540 | tf_op jit(solution)/shard_map/add | solution.py:29
  37.8 4.3 %shift-left_add_fusion.6 = s32[128]{0:T(128)S(1)} fusion(s32[]{:T(128)} %bitcast.89, s32[]{:T(128)} %bitcast.88, s32[]{:T(128)} %bitcast.87, s32[]{:T(128)} %bitcast.86, s32[]{:T(128)} %bitcast.85, s32[]{:T(128)} %bitcast.84, s32[]{:T(128)} %bitcast.83), kind=kLoop, calls=%fused_computation.159 | loop fusion | flops 3456 | bytes 540 | tf_op jit(solution)/shard_map/add | solution.py:29
  42.1 5.6 %shift-left_add_fusion.2 = s32[512]{0:T(512)S(1)} fusion(s32[]{:T(128)} %bitcast.82, s32[]{:T(128)} %bitcast.81, s32[]{:T(128)} %bitcast.80, s32[]{:T(128)} %bitcast.79, s32[]{:T(128)} %bitcast.78, s32[]{:T(128)} %bitcast.77, s32[]{:T(128)} %bitcast.76, s32[]{:T(128)} %bitcast.75, s32[]{:T(128)} %bitcast.74), kind=kLoop, calls=%fused_computation.127 | loop fusion | flops 17920 | bytes 2084 | tf_op jit(solution)/shard_map/add | solution.py:29
  47.7 5.6 %shift-left_add_fusion = s32[512]{0:T(512)S(1)} fusion(s32[]{:T(128)} %bitcast.120, s32[]{:T(128)} %bitcast.119, s32[]{:T(128)} %bitcast.118, s32[]{:T(128)} %bitcast.117, s32[]{:T(128)} %bitcast.116, s32[]{:T(128)} %bitcast.115, s32[]{:T(128)} %bitcast.114, s32[]{:T(128)} %bitcast.113, s32[]{:T(128)} %bitcast.112), kind=kLoop, calls=%fused_computation.125 | loop fusion | flops 17920 | bytes 2084 | tf_op jit(solution)/shard_map/add | solution.py:29
  53.3 5.4 %shift-left_add_fusion.3 = s32[512]{0:T(512)S(1)} fusion(s32[]{:T(128)} %bitcast.66, s32[]{:T(128)} %bitcast.65, s32[]{:T(128)} %bitcast.64, s32[]{:T(128)} %bitcast.63, s32[]{:T(128)} %bitcast.62, s32[]{:T(128)} %bitcast.61, s32[]{:T(128)} %bitcast.60, s32[]{:T(128)} %bitcast.59, s32[]{:T(128)} %bitcast.58), kind=kLoop, calls=%fused_computation.128 | loop fusion | flops 17920 | bytes 2084 | tf_op jit(solution)/shard_map/add | solution.py:29
  58.8 4.3 %shift-left_add_fusion.7 = s32[128]{0:T(128)S(1)} fusion(s32[]{:T(128)} %bitcast.73, s32[]{:T(128)} %bitcast.72, s32[]{:T(128)} %bitcast.71, s32[]{:T(128)} %bitcast.70, s32[]{:T(128)} %bitcast.69, s32[]{:T(128)} %bitcast.68, s32[]{:T(128)} %bitcast.67), kind=kLoop, calls=%fused_computation.160 | loop fusion | flops 3456 | bytes 540 | tf_op jit(solution)/shard_map/add | solution.py:29
  68.1 5.6 %shift-left_add_fusion.1 = s32[512]{0:T(512)S(1)} fusion(s32[]{:T(128)} %bitcast.104, s32[]{:T(128)} %bitcast.103, s32[]{:T(128)} %bitcast.102, s32[]{:T(128)} %bitcast.101, s32[]{:T(128)} %bitcast.100, s32[]{:T(128)} %bitcast.99, s32[]{:T(128)} %bitcast.98, s32[]{:T(128)} %bitcast.97, s32[]{:T(128)} %bitcast.96), kind=kLoop, calls=%fused_computation.126 | loop fusion | flops 17920 | bytes 2084 | tf_op jit(solution)/shard_map/add | solution.py:29
  74.9 9.8 %collective-permute-done.2 = f32[2,32,3072]{2,1,0:T(8,128)} collective-permute-done((f32[2,32,3072]{2,1,0:T(8,128)}, f32[2,32,3072]{2,1,0:T(8,128)}, u32[]{:S(2)}, u32[]{:S(2)}) %collective-permute-start.2) | collective-permute-done | bytes 786464 | tf_op jit(solution)/shard_map/ppermute | solution.py:184
  87.2 4.4 %shift-left_add_fusion.5 = s32[128]{0:T(128)S(1)} fusion(s32[]{:T(128)} %bitcast.111, s32[]{:T(128)} %bitcast.110, s32[]{:T(128)} %bitcast.109, s32[]{:T(128)} %bitcast.108, s32[]{:T(128)} %bitcast.107, s32[]{:T(128)} %bitcast.106, s32[]{:T(128)} %bitcast.105), kind=kLoop, calls=%fused_computation.155 | loop fusion | flops 3456 | bytes 540 | tf_op jit(solution)/shard_map/add | solution.py:29
  119.1 13.1 %collective-permute-done.6 = f32[2,32,3072]{2,1,0:T(8,128)S(1)} collective-permute-done((f32[2,32,3072]{2,1,0:T(8,128)}, f32[2,32,3072]{2,1,0:T(8,128)S(1)}, u32[]{:S(2)}, u32[]{:S(2)}) %collective-permute-start.6) | collective-permute-done | bytes 786464 | tf_op jit(solution)/shard_map/ppermute | solution.py:184
  138.1 11.8 %collective-permute-done.8 = f32[2,32,3072]{2,1,0:T(8,128)S(1)} collective-permute-done((f32[2,32,3072]{2,1,0:T(8,128)S(1)}, f32[2,32,3072]{2,1,0:T(8,128)S(1)}, u32[]{:S(2)}, u32[]{:S(2)}) %collective-permute-start.8) | collective-permute-done | bytes 786464 | tf_op jit(solution)/shard_map/ppermute | solution.py:184
  153.6 14.0 %collective-permute-done.10 = f32[2,32,3072]{2,1,0:T(8,128)S(1)} collective-permute-done((f32[2,32,3072]{2,1,0:T(8,128)S(1)}, f32[2,32,3072]{2,1,0:T(8,128)S(1)}, u32[]{:S(2)}, u32[]{:S(2)}) %collective-permute-start.10) | collective-permute-done | bytes 786464 | tf_op jit(solution)/shard_map/ppermute | solution.py:184
  171.3 11.3 %collective-permute-done.12 = f32[2,32,3072]{2,1,0:T(8,128)S(1)} collective-permute-done((f32[2,32,3072]{2,1,0:T(8,128)S(1)}, f32[2,32,3072]{2,1,0:T(8,128)S(1)}, u32[]{:S(2)}, u32[]{:S(2)}) %collective-permute-start.12) | collective-permute-done | bytes 786464 | tf_op jit(solution)/shard_map/ppermute | solution.py:184
  185.1 5.3 %fusion.2 = f32[512,512]{1,0:T(8,128)S(1)} fusion(f32[2,512,3072]{2,1,0:T(8,128)S(1)} %bitcast.266, f32[2,512,3072]{2,1,0:T(8,128)S(1)} %constant_dynamic-update-slice_fusion), kind=kOutput, calls=%fused_computation.17 | convolution fusion | flops 4831838208 | bytes 13631488 | tf_op jit(solution)/shard_map/dot_general | solution.py:11
  190.5 5.3 %fusion = f32[512,512]{1,0:T(8,128)S(1)} fusion(f32[2,512,3072]{2,1,0:T(8,128)S(1)} %bitcast.266, f32[2,512,3072]{2,1,0:T(8,128)S(1)} %constant_dynamic-update-slice_fusion), kind=kOutput, calls=%fused_computation.15 | convolution fusion | flops 4831838208 | bytes 13631488 | tf_op jit(solution)/shard_map/dot_general | solution.py:11
  195.8 17.5 %fusion.25 = f32[1,512,512]{1,2,0:T(8,128)S(1)} fusion(f32[512,512]{1,0:T(8,128)S(1)} %fusion.2, f32[2,512,3072]{2,1,0:T(8,128)S(1)} %bitcast.266, f32[2,512,3072]{2,1,0:T(8,128)S(1)} %constant_dynamic-update-slice_fusion), kind=kOutput, calls=%fused_computation.37 | convolution fusion | flops 4832100352 | bytes 14680064 | tf_op jit(solution)/shard_map/dot_general | solution.py:11
  213.4 5.3 %fusion.35 = f32[1,512,512]{1,2,0:T(8,128)S(1)} fusion(f32[512,512]{1,0:T(8,128)S(1)} %fusion, f32[2,512,3072]{2,1,0:T(8,128)S(1)} %bitcast.266, f32[2,512,3072]{2,1,0:T(8,128)S(1)} %constant_dynamic-update-slice_fusion), kind=kOutput, calls=%fused_computation.39 | convolution fusion | flops 4832100352 | bytes 14680064 | tf_op jit(solution)/shard_map/dot_general | solution.py:11
  220.8 31.1 %reduce-scatter.2.cloned.1.call-done = f32[2,512,128]{1,2,0:T(8,128)} async-done(((f32[2,512,512]{1,2,0:T(8,128)}), f32[2,512,128]{1,2,0:T(8,128)}) %reduce-scatter.2.cloned.1.call-update) | async-done | bytes 524304 | tf_op jit(solution)/shard_map/reduce_scatter | solution.py:200
  255.0 11.4 %conditional.2 = (f32[2,512,128]{2,1,0:T(8,128)S(1)}) conditional(s32[]{:T(128)} %clamp.7, f32[2,512,128]{2,1,0:T(8,128)S(1)} %fusion.54, f32[2,512,128]{2,1,0:T(8,128)S(1)} %fusion.54, f32[2,512,128]{2,1,0:T(8,128)S(1)} %fusion.54, f32[2,512,128]{2,1,0:T(8,128)S(1)} %fusion.54, ...), branch_computations={%region_23.24_spmd, %region_24.25_spmd, %region_25.26_spmd, %regio... | conditional | bytes 5242888 | solution.py:51
  257.6 5.2 %copy.121 = f32[2,64,8,8,16]{4,3,2,1,0:T(8,128)} copy(f32[2,64,8,8,16]{4,2,3,1,0:T(8,128)} %bitcast.273) | data formatting | bytes 1048576 | tf_op jit(solution)/shard_map/cond/branch_3_fun/transpose | solution.py:46
  262.8 3.2 %reshape.442 = f32[2,512,128]{2,1,0:T(8,128)S(1)} reshape(f32[2,64,8,8,16]{4,3,2,1,0:T(8,128)} %copy.121) | data formatting | bytes 1048576 | tf_op jit(solution)/shard_map/cond/branch_3_fun/reshape | solution.py:47
  271.9 4.8 %all-to-all-start = ((f32[2,32,2048]{2,0,1:T(2,128)}), f32[2,32,2048]{2,0,1:T(2,128)S(1)}, u32[]{:S(2)}, u32[]{:S(2)}) async-start(f32[2,32,2048]{2,0,1:T(2,128)} %copy.145), calls=%async_computation.1 | async-start | bytes 1048576 | tf_op jit(solution)/shard_map/all_to_all | solution.py:163
  277.3 15.6 %all-to-all-done = f32[2,32,2048]{2,0,1:T(2,128)S(1)} async-done(((f32[2,32,2048]{2,0,1:T(2,128)}), f32[2,32,2048]{2,0,1:T(2,128)S(1)}, u32[]{:S(2)}, u32[]{:S(2)}) %all-to-all-start) | async-done | bytes 524320 | tf_op jit(solution)/shard_map/all_to_all | solution.py:163
  297.4 4.9 %conditional.3 = (f32[2,512,128]{2,1,0:T(8,128)S(1)}) conditional(s32[]{:T(128)} %clamp.6, f32[2,512,128]{2,1,0:T(8,128)S(1)} %fusion.50, f32[2,512,128]{2,1,0:T(8,128)S(1)} %fusion.50, f32[2,512,128]{2,1,0:T(8,128)S(1)} %fusion.50, f32[2,512,128]{2,1,0:T(8,128)S(1)} %fusion.50, ...), branch_computations={%region_31.32_spmd, %region_32.33_spmd, %region_33.34_spmd, %regio... | conditional | bytes 5242888 | solution.py:51
  (141 shorter events, 83.2 us)
Async XLA Ops:
  6.5 6.2 %copy-start = (s32[21]{0:T(128)S(1)}, s32[21]{0:T(128)}, u32[]{:S(2)}) copy-start(s32[21]{0:T(128)} %param.28) | copy-start | bytes 256
  6.5 96.4 %copy-start.5 = (s32[8]{0:T(128)S(1)}, s32[8]{0:T(128)}, u32[]{:S(2)}) copy-start(s32[8]{0:T(128)} %constant.222.clone) | copy-start | bytes 100
  6.5 107.4 %copy-start.2 = (f32[2,64,3072]{2,1,0:T(8,128)S(1)}, f32[2,64,3072]{2,1,0:T(8,128)}, u32[]{:S(2)}) copy-start(f32[2,64,3072]{2,1,0:T(8,128)} %param.27) | copy-start | bytes 4718596
  6.5 245.4 %reduce-scatter.2.cloned.1.call-start = ((), (), s32[]{:S(2)}) async-start(), calls=%async_computation.2 | async-start | bytes 2621440 | tf_op jit(solution)/shard_map/reduce_scatter | solution.py:200
  9.1 56.4 %collective-permute-start = (f32[2,32,3072]{2,1,0:T(8,128)}, f32[2,32,3072]{2,1,0:T(8,128)}, u32[]{:S(2)}, u32[]{:S(2)}) collective-permute-start(f32[2,32,3072]{2,1,0:T(8,128)} %get-tuple-element.70), channel_id=1, source_target_pairs={{0,2},{2,4},{4,6},{6,7},{7,5},{5,3},{3,1},{1,0},{8,10},{10,12},{12... | collective-permute-start | bytes 2359304 | tf_op jit(solution)/shard_map/ppermute | solution.py:184
  12.1 56.0 %collective-permute-start.1 = (f32[2,32,3072]{2,1,0:T(8,128)S(1)}, f32[2,32,3072]{2,1,0:T(8,128)S(1)}, u32[]{:S(2)}, u32[]{:S(2)}) collective-permute-start(f32[2,32,3072]{2,1,0:T(8,128)S(1)} %get-tuple-element.69), channel_id=1, source_target_pairs={{2,0},{4,2},{6,4},{7,6},{5,7},{3,5},{1,3},{0,1},{10,8},{12,10},{14... | collective-permute-start | bytes 2359304 | tf_op jit(solution)/shard_map/ppermute | solution.py:185
  65.4 19.3 %collective-permute-start.2 = (f32[2,32,3072]{2,1,0:T(8,128)}, f32[2,32,3072]{2,1,0:T(8,128)}, u32[]{:S(2)}, u32[]{:S(2)}) collective-permute-start(f32[2,32,3072]{2,1,0:T(8,128)} %collective-permute-done), channel_id=1, source_target_pairs={{0,2},{2,4},{4,6},{6,7},{7,5},{5,3},{3,1},{1,0},{8,10},{10,12},{12... | collective-permute-start | bytes 2359304 | tf_op jit(solution)/shard_map/ppermute | solution.py:184
  68.1 23.5 %collective-permute-start.3 = (f32[2,32,3072]{2,1,0:T(8,128)S(1)}, f32[2,32,3072]{2,1,0:T(8,128)}, u32[]{:S(2)}, u32[]{:S(2)}) collective-permute-start(f32[2,32,3072]{2,1,0:T(8,128)S(1)} %collective-permute-done.1), channel_id=1, source_target_pairs={{2,0},{4,2},{6,4},{7,6},{5,7},{3,5},{1,3},{0,1},{10,8},{12,10},{14... | collective-permute-start | bytes 2359304 | tf_op jit(solution)/shard_map/ppermute | solution.py:185
  84.8 29.4 %collective-permute-start.4 = (f32[2,32,3072]{2,1,0:T(8,128)}, f32[2,32,3072]{2,1,0:T(8,128)}, u32[]{:S(2)}, u32[]{:S(2)}) collective-permute-start(f32[2,32,3072]{2,1,0:T(8,128)} %collective-permute-done.2), channel_id=1, source_target_pairs={{0,2},{2,4},{4,6},{6,7},{7,5},{5,3},{3,1},{1,0},{8,10},{10,12},{12... | collective-permute-start | bytes 2359304 | tf_op jit(solution)/shard_map/ppermute | solution.py:184
  91.6 25.6 %collective-permute-start.5 = (f32[2,32,3072]{2,1,0:T(8,128)}, f32[2,32,3072]{2,1,0:T(8,128)}, u32[]{:S(2)}, u32[]{:S(2)}) collective-permute-start(f32[2,32,3072]{2,1,0:T(8,128)} %collective-permute-done.3), channel_id=1, source_target_pairs={{2,0},{4,2},{6,4},{7,6},{5,7},{3,5},{1,3},{0,1},{10,8},{12,10},{14... | collective-permute-start | bytes 2359304 | tf_op jit(solution)/shard_map/ppermute | solution.py:185
  114.0 71.1 %slice-start = ((s8[12582912]{0:T(1024)(128)(4,1)}), s8[4194304]{0:T(1024)(128)(4,1)S(1)}, s32[]{:S(2)}) async-start(s8[12582912]{0:T(1024)(128)(4,1)} %bitcast.265), calls=%async_computation.3 | async-start | bytes 8388608
  114.2 18.0 %collective-permute-start.6 = (f32[2,32,3072]{2,1,0:T(8,128)}, f32[2,32,3072]{2,1,0:T(8,128)S(1)}, u32[]{:S(2)}, u32[]{:S(2)}) collective-permute-start(f32[2,32,3072]{2,1,0:T(8,128)} %collective-permute-done.4), channel_id=1, source_target_pairs={{0,2},{2,4},{4,6},{6,7},{7,5},{5,3},{3,1},{1,0},{8,10},{10,12},{12... | collective-permute-start | bytes 2359304 | tf_op jit(solution)/shard_map/ppermute | solution.py:184
  117.2 17.9 %collective-permute-start.7 = (f32[2,32,3072]{2,1,0:T(8,128)}, f32[2,32,3072]{2,1,0:T(8,128)S(1)}, u32[]{:S(2)}, u32[]{:S(2)}) collective-permute-start(f32[2,32,3072]{2,1,0:T(8,128)} %collective-permute-done.5), channel_id=1, source_target_pairs={{2,0},{4,2},{6,4},{7,6},{5,7},{3,5},{1,3},{0,1},{10,8},{12,10},{14... | collective-permute-start | bytes 2359304 | tf_op jit(solution)/shard_map/ppermute | solution.py:185
  119.1 66.0 %slice-start.1 = ((s8[12582912]{0:T(1024)(128)(4,1)}), s8[4194304]{0:T(1024)(128)(4,1)S(1)}, s32[]{:S(2)}) async-start(s8[12582912]{0:T(1024)(128)(4,1)} %bitcast.265), calls=%async_computation.4 | async-start | bytes 8388608
  132.1 17.7 %collective-permute-start.8 = (f32[2,32,3072]{2,1,0:T(8,128)S(1)}, f32[2,32,3072]{2,1,0:T(8,128)S(1)}, u32[]{:S(2)}, u32[]{:S(2)}) collective-permute-start(f32[2,32,3072]{2,1,0:T(8,128)S(1)} %collective-permute-done.6), channel_id=1, source_target_pairs={{0,2},{2,4},{4,6},{6,7},{7,5},{5,3},{3,1},{1,0},{8,10},{10,12},{12... | collective-permute-start | bytes 2359304 | tf_op jit(solution)/shard_map/ppermute | solution.py:184
  135.1 17.8 %collective-permute-start.9 = (f32[2,32,3072]{2,1,0:T(8,128)S(1)}, f32[2,32,3072]{2,1,0:T(8,128)S(1)}, u32[]{:S(2)}, u32[]{:S(2)}) collective-permute-start(f32[2,32,3072]{2,1,0:T(8,128)S(1)} %collective-permute-done.7), channel_id=1, source_target_pairs={{2,0},{4,2},{6,4},{7,6},{5,7},{3,5},{1,3},{0,1},{10,8},{12,10},{14... | collective-permute-start | bytes 2359304 | tf_op jit(solution)/shard_map/ppermute | solution.py:185
  149.9 17.7 %collective-permute-start.10 = (f32[2,32,3072]{2,1,0:T(8,128)S(1)}, f32[2,32,3072]{2,1,0:T(8,128)S(1)}, u32[]{:S(2)}, u32[]{:S(2)}) collective-permute-start(f32[2,32,3072]{2,1,0:T(8,128)S(1)} %collective-permute-done.8), channel_id=1, source_target_pairs={{0,2},{2,4},{4,6},{6,7},{7,5},{5,3},{3,1},{1,0},{8,10},{10,12},{12... | collective-permute-start | bytes 2359304 | tf_op jit(solution)/shard_map/ppermute | solution.py:184
  152.8 17.5 %collective-permute-start.11 = (f32[2,32,3072]{2,1,0:T(8,128)S(1)}, f32[2,32,3072]{2,1,0:T(8,128)S(1)}, u32[]{:S(2)}, u32[]{:S(2)}) collective-permute-start(f32[2,32,3072]{2,1,0:T(8,128)S(1)} %collective-permute-done.9), channel_id=1, source_target_pairs={{2,0},{4,2},{6,4},{7,6},{5,7},{3,5},{1,3},{0,1},{10,8},{12,10},{14... | collective-permute-start | bytes 2359304 | tf_op jit(solution)/shard_map/ppermute | solution.py:185
  153.5 31.6 %slice-start.2 = ((s8[12582912]{0:T(1024)(128)(4,1)}), s8[4194304]{0:T(1024)(128)(4,1)S(1)}, s32[]{:S(2)}) async-start(s8[12582912]{0:T(1024)(128)(4,1)} %bitcast.265), calls=%async_computation.5 | async-start | bytes 8388608
  167.6 15.0 %collective-permute-start.12 = (f32[2,32,3072]{2,1,0:T(8,128)S(1)}, f32[2,32,3072]{2,1,0:T(8,128)S(1)}, u32[]{:S(2)}, u32[]{:S(2)}) collective-permute-start(f32[2,32,3072]{2,1,0:T(8,128)S(1)} %collective-permute-done.10), channel_id=1, source_target_pairs={{0,2},{2,4},{4,6},{6,7},{7,5},{5,3},{3,1},{1,0},{8,10},{10,12},{12... | collective-permute-start | bytes 2359304 | tf_op jit(solution)/shard_map/ppermute | solution.py:184
  170.3 14.7 %collective-permute-start.13 = (f32[2,32,3072]{2,1,0:T(8,128)S(1)}, f32[2,32,3072]{2,1,0:T(8,128)S(1)}, u32[]{:S(2)}, u32[]{:S(2)}) collective-permute-start(f32[2,32,3072]{2,1,0:T(8,128)S(1)} %collective-permute-done.11), channel_id=1, source_target_pairs={{2,0},{4,2},{6,4},{7,6},{5,7},{3,5},{1,3},{0,1},{10,8},{12,10},{14... | collective-permute-start | bytes 2359304 | tf_op jit(solution)/shard_map/ppermute | solution.py:185
  213.4 40.7 %copy-start.4 = (f32[128,128]{1,0:T(8,128)S(1)}, f32[128,128]{1,0:T(8,128)}, u32[]{:S(2)}) copy-start(f32[128,128]{1,0:T(8,128)} %fusion.56) | copy-start | bytes 196612
  255.0 41.4 %copy-start.3 = (f32[128,128]{1,0:T(8,128)S(1)}, f32[128,128]{1,0:T(8,128)}, u32[]{:S(2)}) copy-start(f32[128,128]{1,0:T(8,128)} %fusion.58) | copy-start | bytes 196612
  271.9 21.0 %all-to-all-start = ((f32[2,32,2048]{2,0,1:T(2,128)}), f32[2,32,2048]{2,0,1:T(2,128)S(1)}, u32[]{:S(2)}, u32[]{:S(2)}) async-start(f32[2,32,2048]{2,0,1:T(2,128)} %copy.145), calls=%async_computation.1 | async-start | bytes 1048576 | tf_op jit(solution)/shard_map/all_to_all | solution.py:163
  (1 other events, 5.0 us)
Sparse Core Ops, SparseCore 0:
  220.4 31.4 reduce-scatter.1
where the time goes:
time: 312 us; the launch traced here: 315 us
  waiting for transfers between devices  111 us (36%)
  other arithmetic  50.4 us (16%)
  matrix products  49.9 us (16%)
  local copies, waits for them, and re-layouts  43.1 us (14%)
  between operations  34.5 us (11%)
  starting transfers between devices  21.6 us (7%)
  loops' own time  3.82 us (1%)
    ppermute x7, waiting for transfers between devices, ring_all_gather(): ahead = lax.ppermute(ahead, axis, fwd)  60 us
    add x8, other arithmetic, perm_matrix(): moved + jnp.left_shift(jnp.right_shift(old, bit_num) & 1, new_pos[bit_num])  39.5 us
    dot_general x4, matrix products, cross_dot(): lax.dot_general(left, right, (((1,), (1,)), ((), ())), precision=lax.Prec...  33.6 us
    reduce_scatter x1, waiting for transfers between devices, per_device(): lax.psum_scatter(partial_sums, 'bond', scatter_dimension=2, tiled=True)  31.1 us
    all_to_all x1, waiting for transfers between devices, regroup(): lax.all_to_all(block, ('bond', 'rows'), split_axis=1, concat_axis=1, tile...  15.6 us
    ppermute x7, starting transfers between devices, ring_all_gather(): ahead = lax.ppermute(ahead, axis, fwd)  13.8 us
    dot_general x4, matrix products, permute_rows(): jnp.einsum('no,pol->pnl', mat, block, precision=lax.Precision.HIGHEST)  11.6 us
  transfers between devices with their start and end apart: 16, of which 10 were waited for; matrix products, arithmetic and copies ran while one was open for 24% of the time, Pallas kernels for 0%

commit v1 on v0

--- a/solution.py
+++ b/solution.py
@@ -27,6 +27,7 @@
     moved = jnp.zeros_like(old)
     for bit_num in range(nbits):
         moved = moved + jnp.left_shift(jnp.right_shift(old, bit_num) & 1, new_pos[bit_num])
+    moved = lax.optimization_barrier(moved)
     return (old[:, None] == moved[None, :]).astype(jnp.float32)
 
 

time: 312 us -> 324 us (1.038); the launches traced: 315 us -> 330 us
  local copies, waits for them, and re-layouts: 43.1 us -> 56.1 us
    transpose x2, local copies, waits for them, and re-layouts: 5.88 us -> 12 us  [run(): x = jnp.transpose(x, (0, 1, 3, 2, 4))]
    reshape x3, local copies, waits for them, and re-layouts: 3.7 us -> 7.93 us  [run(): return x.reshape(planes, 2 ** rbits, 2 ** cbits)]
  transfers between devices with their start and end apart: 16 -> 16, of which waited for: 10 -> 10; matrix products, arithmetic and copies ran while one was open for 24% -> 23% of each run, Pallas kernels for 0% -> 0%
where the time goes in v1:
time: 324 us; the launch traced here: 330 us
  waiting for transfers between devices  113 us (35%)
  local copies, waits for them, and re-layouts  56.1 us (17%)
  other arithmetic  51 us (16%)
  matrix products  49.9 us (15%)
  between operations  34.5 us (11%)
  starting transfers between devices  21.6 us (7%)
  loops' own time  3.79 us (1%)
    ppermute x7, waiting for transfers between devices, ring_all_gather(): ahead = lax.ppermute(ahead, axis, fwd)  61.8 us
    add x8, other arithmetic, perm_matrix(): moved + jnp.left_shift(jnp.right_shift(old, bit_num) & 1, new_pos[bit_num])  40.1 us
    dot_general x4, matrix products, cross_dot(): lax.dot_general(left, right, (((1,), (1,)), ((), ())), precision=lax.Prec...  33.6 us
    reduce_scatter x1, waiting for transfers between devices, per_device(): lax.psum_scatter(partial_sums, 'bond', scatter_dimension=2, tiled=True)  31.1 us
    all_to_all x1, waiting for transfers between devices, regroup(): lax.all_to_all(block, ('bond', 'rows'), split_axis=1, concat_axis=1, tile...  15.6 us
    ppermute x7, starting transfers between devices, ring_all_gather(): ahead = lax.ppermute(ahead, axis, fwd)  13.8 us
    transpose x2, local copies, waits for them, and re-layouts, run(): x = jnp.transpose(x, (0, 1, 3, 2, 4))  12 us
    dot_general x4, matrix products, permute_rows(): jnp.einsum('no,pol->pnl', mat, block, precision=lax.Precision.HIGHEST)  11.6 us
  transfers between devices with their start and end apart: 16, of which 10 were waited for; matrix products, arithmetic and copies ran while one was open for 23% of the time, Pallas kernels for 0%

profile of v1, /device:TPU:0, one launch (start us, length us, event | category | flops | bytes accessed | tf_op | source)
XLA Modules:
  0.0 329.8 jit_solution(13026132198014518234)
XLA Ops:
  27.6 5.6 %shift-left_add_fusion.2 = s32[512]{0:T(512)S(1)} fusion(s32[]{:T(128)} %bitcast.82, s32[]{:T(128)} %bitcast.81, s32[]{:T(128)} %bitcast.80, s32[]{:T(128)} %bitcast.79, s32[]{:T(128)} %bitcast.78, s32[]{:T(128)} %bitcast.77, s32[]{:T(128)} %bitcast.76, s32[]{:T(128)} %bitcast.75, s32[]{:T(128)} %bitcast.74), kind=kLoop, calls=%fused_computation.127 | loop fusion | flops 17920 | bytes 2084 | tf_op jit(solution)/shard_map/add | solution.py:29
  34.6 5.6 %shift-left_add_fusion = s32[512]{0:T(512)S(1)} fusion(s32[]{:T(128)} %bitcast.120, s32[]{:T(128)} %bitcast.119, s32[]{:T(128)} %bitcast.118, s32[]{:T(128)} %bitcast.117, s32[]{:T(128)} %bitcast.116, s32[]{:T(128)} %bitcast.115, s32[]{:T(128)} %bitcast.114, s32[]{:T(128)} %bitcast.113, s32[]{:T(128)} %bitcast.112), kind=kLoop, calls=%fused_computation.125 | loop fusion | flops 17920 | bytes 2084 | tf_op jit(solution)/shard_map/add | solution.py:29
  40.9 5.6 %shift-left_add_fusion.3 = s32[512]{0:T(512)S(1)} fusion(s32[]{:T(128)} %bitcast.66, s32[]{:T(128)} %bitcast.65, s32[]{:T(128)} %bitcast.64, s32[]{:T(128)} %bitcast.63, s32[]{:T(128)} %bitcast.62, s32[]{:T(128)} %bitcast.61, s32[]{:T(128)} %bitcast.60, s32[]{:T(128)} %bitcast.59, s32[]{:T(128)} %bitcast.58), kind=kLoop, calls=%fused_computation.128 | loop fusion | flops 17920 | bytes 2084 | tf_op jit(solution)/shard_map/add | solution.py:29
  47.3 5.6 %shift-left_add_fusion.1 = s32[512]{0:T(512)S(1)} fusion(s32[]{:T(128)} %bitcast.104, s32[]{:T(128)} %bitcast.103, s32[]{:T(128)} %bitcast.102, s32[]{:T(128)} %bitcast.101, s32[]{:T(128)} %bitcast.100, s32[]{:T(128)} %bitcast.99, s32[]{:T(128)} %bitcast.98, s32[]{:T(128)} %bitcast.97, s32[]{:T(128)} %bitcast.96), kind=kLoop, calls=%fused_computation.126 | loop fusion | flops 17920 | bytes 2084 | tf_op jit(solution)/shard_map/add | solution.py:29
  54.2 4.4 %shift-left_add_fusion.4 = s32[128]{0:T(128)S(1)} fusion(s32[]{:T(128)} %bitcast.127, s32[]{:T(128)} %bitcast.126, s32[]{:T(128)} %bitcast.125, s32[]{:T(128)} %bitcast.124, s32[]{:T(128)} %bitcast.123, s32[]{:T(128)} %bitcast.122, s32[]{:T(128)} %bitcast.121), kind=kLoop, calls=%fused_computation.154 | loop fusion | flops 3456 | bytes 540 | tf_op jit(solution)/shard_map/add | solution.py:29
  59.9 4.4 %shift-left_add_fusion.6 = s32[128]{0:T(128)S(1)} fusion(s32[]{:T(128)} %bitcast.89, s32[]{:T(128)} %bitcast.88, s32[]{:T(128)} %bitcast.87, s32[]{:T(128)} %bitcast.86, s32[]{:T(128)} %bitcast.85, s32[]{:T(128)} %bitcast.84, s32[]{:T(128)} %bitcast.83), kind=kLoop, calls=%fused_computation.159 | loop fusion | flops 3456 | bytes 540 | tf_op jit(solution)/shard_map/add | solution.py:29
  65.0 4.4 %shift-left_add_fusion.7 = s32[128]{0:T(128)S(1)} fusion(s32[]{:T(128)} %bitcast.73, s32[]{:T(128)} %bitcast.72, s32[]{:T(128)} %bitcast.71, s32[]{:T(128)} %bitcast.70, s32[]{:T(128)} %bitcast.69, s32[]{:T(128)} %bitcast.68, s32[]{:T(128)} %bitcast.67), kind=kLoop, calls=%fused_computation.160 | loop fusion | flops 3456 | bytes 540 | tf_op jit(solution)/shard_map/add | solution.py:29
  80.1 11.6 %collective-permute-done.2 = f32[2,32,3072]{2,1,0:T(8,128)} collective-permute-done((f32[2,32,3072]{2,1,0:T(8,128)}, f32[2,32,3072]{2,1,0:T(8,128)}, u32[]{:S(2)}, u32[]{:S(2)}) %collective-permute-start.2) | collective-permute-done | bytes 786464 | tf_op jit(solution)/shard_map/ppermute | solution.py:185
  121.5 13.1 %collective-permute-done.6 = f32[2,32,3072]{2,1,0:T(8,128)S(1)} collective-permute-done((f32[2,32,3072]{2,1,0:T(8,128)}, f32[2,32,3072]{2,1,0:T(8,128)S(1)}, u32[]{:S(2)}, u32[]{:S(2)}) %collective-permute-start.6) | collective-permute-done | bytes 786464 | tf_op jit(solution)/shard_map/ppermute | solution.py:185
  140.6 11.8 %collective-permute-done.8 = f32[2,32,3072]{2,1,0:T(8,128)S(1)} collective-permute-done((f32[2,32,3072]{2,1,0:T(8,128)S(1)}, f32[2,32,3072]{2,1,0:T(8,128)S(1)}, u32[]{:S(2)}, u32[]{:S(2)}) %collective-permute-start.8) | collective-permute-done | bytes 786464 | tf_op jit(solution)/shard_map/ppermute | solution.py:185
  156.0 14.0 %collective-permute-done.10 = f32[2,32,3072]{2,1,0:T(8,128)S(1)} collective-permute-done((f32[2,32,3072]{2,1,0:T(8,128)S(1)}, f32[2,32,3072]{2,1,0:T(8,128)S(1)}, u32[]{:S(2)}, u32[]{:S(2)}) %collective-permute-start.10) | collective-permute-done | bytes 786464 | tf_op jit(solution)/shard_map/ppermute | solution.py:185
  173.7 11.3 %collective-permute-done.12 = f32[2,32,3072]{2,1,0:T(8,128)S(1)} collective-permute-done((f32[2,32,3072]{2,1,0:T(8,128)S(1)}, f32[2,32,3072]{2,1,0:T(8,128)S(1)}, u32[]{:S(2)}, u32[]{:S(2)}) %collective-permute-start.12) | collective-permute-done | bytes 786464 | tf_op jit(solution)/shard_map/ppermute | solution.py:185
  187.6 5.3 %fusion.2 = f32[512,512]{1,0:T(8,128)S(1)} fusion(f32[2,512,3072]{2,1,0:T(8,128)S(1)} %bitcast.266, f32[2,512,3072]{2,1,0:T(8,128)S(1)} %constant_dynamic-update-slice_fusion), kind=kOutput, calls=%fused_computation.17 | convolution fusion | flops 4831838208 | bytes 13631488 | tf_op jit(solution)/shard_map/dot_general | solution.py:11
  192.9 5.3 %fusion = f32[512,512]{1,0:T(8,128)S(1)} fusion(f32[2,512,3072]{2,1,0:T(8,128)S(1)} %bitcast.266, f32[2,512,3072]{2,1,0:T(8,128)S(1)} %constant_dynamic-update-slice_fusion), kind=kOutput, calls=%fused_computation.15 | convolution fusion | flops 4831838208 | bytes 13631488 | tf_op jit(solution)/shard_map/dot_general | solution.py:11
  198.3 17.5 %fusion.25 = f32[1,512,512]{1,2,0:T(8,128)S(1)} fusion(f32[512,512]{1,0:T(8,128)S(1)} %fusion.2, f32[2,512,3072]{2,1,0:T(8,128)S(1)} %bitcast.266, f32[2,512,3072]{2,1,0:T(8,128)S(1)} %constant_dynamic-update-slice_fusion), kind=kOutput, calls=%fused_computation.37 | convolution fusion | flops 4832100352 | bytes 14680064 | tf_op jit(solution)/shard_map/dot_general | solution.py:11
  215.8 5.3 %fusion.35 = f32[1,512,512]{1,2,0:T(8,128)S(1)} fusion(f32[512,512]{1,0:T(8,128)S(1)} %fusion, f32[2,512,3072]{2,1,0:T(8,128)S(1)} %bitcast.266, f32[2,512,3072]{2,1,0:T(8,128)S(1)} %constant_dynamic-update-slice_fusion), kind=kOutput, calls=%fused_computation.39 | convolution fusion | flops 4832100352 | bytes 14680064 | tf_op jit(solution)/shard_map/dot_general | solution.py:11
  223.3 31.1 %reduce-scatter.2.cloned.1.call-done = f32[2,512,128]{1,2,0:T(8,128)} async-done(((f32[2,512,512]{1,2,0:T(8,128)}), f32[2,512,128]{1,2,0:T(8,128)}) %reduce-scatter.2.cloned.1.call-update) | async-done | bytes 524304 | tf_op jit(solution)/shard_map/reduce_scatter | solution.py:201
  257.5 11.4 %conditional.2 = (f32[2,512,128]{2,1,0:T(8,128)S(1)}) conditional(s32[]{:T(128)} %clamp.7, f32[2,512,128]{2,1,0:T(8,128)S(1)} %fusion.54, f32[2,512,128]{2,1,0:T(8,128)S(1)} %fusion.54, f32[2,512,128]{2,1,0:T(8,128)S(1)} %fusion.54, f32[2,512,128]{2,1,0:T(8,128)S(1)} %fusion.54, ...), branch_computations={%region_23.24_spmd, %region_24.25_spmd, %region_25.26_spmd, %regio... | conditional | bytes 5242888 | solution.py:52
  260.1 5.2 %copy.121 = f32[2,64,8,8,16]{4,3,2,1,0:T(8,128)} copy(f32[2,64,8,8,16]{4,2,3,1,0:T(8,128)} %bitcast.273) | data formatting | bytes 1048576 | tf_op jit(solution)/shard_map/cond/branch_3_fun/transpose | solution.py:47
  274.3 4.8 %all-to-all-start = ((f32[2,32,2048]{2,0,1:T(2,128)}), f32[2,32,2048]{2,0,1:T(2,128)S(1)}, u32[]{:S(2)}, u32[]{:S(2)}) async-start(f32[2,32,2048]{2,0,1:T(2,128)} %copy.145), calls=%async_computation.1 | async-start | bytes 1048576 | tf_op jit(solution)/shard_map/all_to_all | solution.py:164
  279.7 15.6 %all-to-all-done = f32[2,32,2048]{2,0,1:T(2,128)S(1)} async-done(((f32[2,32,2048]{2,0,1:T(2,128)}), f32[2,32,2048]{2,0,1:T(2,128)S(1)}, u32[]{:S(2)}, u32[]{:S(2)}) %all-to-all-start) | async-done | bytes 524320 | tf_op jit(solution)/shard_map/all_to_all | solution.py:164
  299.9 17.8 %conditional.3 = (f32[2,512,128]{2,1,0:T(8,128)S(1)}) conditional(s32[]{:T(128)} %clamp.6, f32[2,512,128]{2,1,0:T(8,128)S(1)} %fusion.50, f32[2,512,128]{2,1,0:T(8,128)S(1)} %fusion.50, f32[2,512,128]{2,1,0:T(8,128)S(1)} %fusion.50, f32[2,512,128]{2,1,0:T(8,128)S(1)} %fusion.50, ...), branch_computations={%region_31.32_spmd, %region_32.33_spmd, %region_33.34_spmd, %regio... | conditional | bytes 5242888 | solution.py:52
  303.1 6.8 %copy.132 = f32[2,32,16,16,8]{2,1,4,3,0:T(8,128)} copy(f32[2,32,16,16,8]{3,1,4,2,0:T(8,128)} %bitcast.272) | data formatting | bytes 1048576 | tf_op jit(solution)/shard_map/cond/branch_4_fun/transpose | solution.py:47
  309.9 4.5 %reshape.282 = f32[2,512,128]{1,2,0:T(8,128)S(1)} reshape(f32[2,32,16,16,8]{2,1,4,3,0:T(8,128)} %copy.132) | data formatting | bytes 1048576 | tf_op jit(solution)/shard_map/cond/branch_4_fun/reshape | solution.py:48
  (141 shorter events, 92.5 us)
Async XLA Ops:
  6.5 6.2 %copy-start = (s32[21]{0:T(128)S(1)}, s32[21]{0:T(128)}, u32[]{:S(2)}) copy-start(s32[21]{0:T(128)} %param.28) | copy-start | bytes 256
  6.5 98.9 %copy-start.5 = (s32[8]{0:T(128)S(1)}, s32[8]{0:T(128)}, u32[]{:S(2)}) copy-start(s32[8]{0:T(128)} %constant.222.clone) | copy-start | bytes 100
  6.5 109.9 %copy-start.2 = (f32[2,64,3072]{2,1,0:T(8,128)S(1)}, f32[2,64,3072]{2,1,0:T(8,128)}, u32[]{:S(2)}) copy-start(f32[2,64,3072]{2,1,0:T(8,128)} %param.27) | copy-start | bytes 4718596
  6.5 247.8 %reduce-scatter.2.cloned.1.call-start = ((), (), s32[]{:S(2)}) async-start(), calls=%async_computation.2 | async-start | bytes 2621440 | tf_op jit(solution)/shard_map/reduce_scatter | solution.py:201
  9.1 63.4 %collective-permute-start = (f32[2,32,3072]{2,1,0:T(8,128)}, f32[2,32,3072]{2,1,0:T(8,128)}, u32[]{:S(2)}, u32[]{:S(2)}) collective-permute-start(f32[2,32,3072]{2,1,0:T(8,128)} %get-tuple-element.70), channel_id=1, source_target_pairs={{0,2},{2,4},{4,6},{6,7},{7,5},{5,3},{3,1},{1,0},{8,10},{10,12},{12... | collective-permute-start | bytes 2359304 | tf_op jit(solution)/shard_map/ppermute | solution.py:185
  12.1 62.4 %collective-permute-start.1 = (f32[2,32,3072]{2,1,0:T(8,128)S(1)}, f32[2,32,3072]{2,1,0:T(8,128)S(1)}, u32[]{:S(2)}, u32[]{:S(2)}) collective-permute-start(f32[2,32,3072]{2,1,0:T(8,128)S(1)} %get-tuple-element.69), channel_id=1, source_target_pairs={{2,0},{4,2},{6,4},{7,6},{5,7},{3,5},{1,3},{0,1},{10,8},{12,10},{14... | collective-permute-start | bytes 2359304 | tf_op jit(solution)/shard_map/ppermute | solution.py:186
  72.4 19.3 %collective-permute-start.2 = (f32[2,32,3072]{2,1,0:T(8,128)}, f32[2,32,3072]{2,1,0:T(8,128)}, u32[]{:S(2)}, u32[]{:S(2)}) collective-permute-start(f32[2,32,3072]{2,1,0:T(8,128)} %collective-permute-done), channel_id=1, source_target_pairs={{0,2},{2,4},{4,6},{6,7},{7,5},{5,3},{3,1},{1,0},{8,10},{10,12},{12... | collective-permute-start | bytes 2359304 | tf_op jit(solution)/shard_map/ppermute | solution.py:185
  74.5 19.7 %collective-permute-start.3 = (f32[2,32,3072]{2,1,0:T(8,128)S(1)}, f32[2,32,3072]{2,1,0:T(8,128)}, u32[]{:S(2)}, u32[]{:S(2)}) collective-permute-start(f32[2,32,3072]{2,1,0:T(8,128)S(1)} %collective-permute-done.1), channel_id=1, source_target_pairs={{2,0},{4,2},{6,4},{7,6},{5,7},{3,5},{1,3},{0,1},{10,8},{12,10},{14... | collective-permute-start | bytes 2359304 | tf_op jit(solution)/shard_map/ppermute | solution.py:186
  91.7 24.9 %collective-permute-start.4 = (f32[2,32,3072]{2,1,0:T(8,128)}, f32[2,32,3072]{2,1,0:T(8,128)}, u32[]{:S(2)}, u32[]{:S(2)}) collective-permute-start(f32[2,32,3072]{2,1,0:T(8,128)} %collective-permute-done.2), channel_id=1, source_target_pairs={{0,2},{2,4},{4,6},{6,7},{7,5},{5,3},{3,1},{1,0},{8,10},{10,12},{12... | collective-permute-start | bytes 2359304 | tf_op jit(solution)/shard_map/ppermute | solution.py:185
  94.1 25.5 %collective-permute-start.5 = (f32[2,32,3072]{2,1,0:T(8,128)}, f32[2,32,3072]{2,1,0:T(8,128)}, u32[]{:S(2)}, u32[]{:S(2)}) collective-permute-start(f32[2,32,3072]{2,1,0:T(8,128)} %collective-permute-done.3), channel_id=1, source_target_pairs={{2,0},{4,2},{6,4},{7,6},{5,7},{3,5},{1,3},{0,1},{10,8},{12,10},{14... | collective-permute-start | bytes 2359304 | tf_op jit(solution)/shard_map/ppermute | solution.py:186
  116.4 71.1 %slice-start = ((s8[12582912]{0:T(1024)(128)(4,1)}), s8[4194304]{0:T(1024)(128)(4,1)S(1)}, s32[]{:S(2)}) async-start(s8[12582912]{0:T(1024)(128)(4,1)} %bitcast.265), calls=%async_computation.3 | async-start | bytes 8388608
  116.6 18.0 %collective-permute-start.6 = (f32[2,32,3072]{2,1,0:T(8,128)}, f32[2,32,3072]{2,1,0:T(8,128)S(1)}, u32[]{:S(2)}, u32[]{:S(2)}) collective-permute-start(f32[2,32,3072]{2,1,0:T(8,128)} %collective-permute-done.4), channel_id=1, source_target_pairs={{0,2},{2,4},{4,6},{6,7},{7,5},{5,3},{3,1},{1,0},{8,10},{10,12},{12... | collective-permute-start | bytes 2359304 | tf_op jit(solution)/shard_map/ppermute | solution.py:185
  119.6 17.9 %collective-permute-start.7 = (f32[2,32,3072]{2,1,0:T(8,128)}, f32[2,32,3072]{2,1,0:T(8,128)S(1)}, u32[]{:S(2)}, u32[]{:S(2)}) collective-permute-start(f32[2,32,3072]{2,1,0:T(8,128)} %collective-permute-done.5), channel_id=1, source_target_pairs={{2,0},{4,2},{6,4},{7,6},{5,7},{3,5},{1,3},{0,1},{10,8},{12,10},{14... | collective-permute-start | bytes 2359304 | tf_op jit(solution)/shard_map/ppermute | solution.py:186
  121.5 66.0 %slice-start.1 = ((s8[12582912]{0:T(1024)(128)(4,1)}), s8[4194304]{0:T(1024)(128)(4,1)S(1)}, s32[]{:S(2)}) async-start(s8[12582912]{0:T(1024)(128)(4,1)} %bitcast.265), calls=%async_computation.4 | async-start | bytes 8388608
  134.6 17.7 %collective-permute-start.8 = (f32[2,32,3072]{2,1,0:T(8,128)S(1)}, f32[2,32,3072]{2,1,0:T(8,128)S(1)}, u32[]{:S(2)}, u32[]{:S(2)}) collective-permute-start(f32[2,32,3072]{2,1,0:T(8,128)S(1)} %collective-permute-done.6), channel_id=1, source_target_pairs={{0,2},{2,4},{4,6},{6,7},{7,5},{5,3},{3,1},{1,0},{8,10},{10,12},{12... | collective-permute-start | bytes 2359304 | tf_op jit(solution)/shard_map/ppermute | solution.py:185
  137.5 17.8 %collective-permute-start.9 = (f32[2,32,3072]{2,1,0:T(8,128)S(1)}, f32[2,32,3072]{2,1,0:T(8,128)S(1)}, u32[]{:S(2)}, u32[]{:S(2)}) collective-permute-start(f32[2,32,3072]{2,1,0:T(8,128)S(1)} %collective-permute-done.7), channel_id=1, source_target_pairs={{2,0},{4,2},{6,4},{7,6},{5,7},{3,5},{1,3},{0,1},{10,8},{12,10},{14... | collective-permute-start | bytes 2359304 | tf_op jit(solution)/shard_map/ppermute | solution.py:186
  152.3 17.7 %collective-permute-start.10 = (f32[2,32,3072]{2,1,0:T(8,128)S(1)}, f32[2,32,3072]{2,1,0:T(8,128)S(1)}, u32[]{:S(2)}, u32[]{:S(2)}) collective-permute-start(f32[2,32,3072]{2,1,0:T(8,128)S(1)} %collective-permute-done.8), channel_id=1, source_target_pairs={{0,2},{2,4},{4,6},{6,7},{7,5},{5,3},{3,1},{1,0},{8,10},{10,12},{12... | collective-permute-start | bytes 2359304 | tf_op jit(solution)/shard_map/ppermute | solution.py:185
  155.3 17.5 %collective-permute-start.11 = (f32[2,32,3072]{2,1,0:T(8,128)S(1)}, f32[2,32,3072]{2,1,0:T(8,128)S(1)}, u32[]{:S(2)}, u32[]{:S(2)}) collective-permute-start(f32[2,32,3072]{2,1,0:T(8,128)S(1)} %collective-permute-done.9), channel_id=1, source_target_pairs={{2,0},{4,2},{6,4},{7,6},{5,7},{3,5},{1,3},{0,1},{10,8},{12,10},{14... | collective-permute-start | bytes 2359304 | tf_op jit(solution)/shard_map/ppermute | solution.py:186
  155.9 31.6 %slice-start.2 = ((s8[12582912]{0:T(1024)(128)(4,1)}), s8[4194304]{0:T(1024)(128)(4,1)S(1)}, s32[]{:S(2)}) async-start(s8[12582912]{0:T(1024)(128)(4,1)} %bitcast.265), calls=%async_computation.5 | async-start | bytes 8388608
  170.0 15.0 %collective-permute-start.12 = (f32[2,32,3072]{2,1,0:T(8,128)S(1)}, f32[2,32,3072]{2,1,0:T(8,128)S(1)}, u32[]{:S(2)}, u32[]{:S(2)}) collective-permute-start(f32[2,32,3072]{2,1,0:T(8,128)S(1)} %collective-permute-done.10), channel_id=1, source_target_pairs={{0,2},{2,4},{4,6},{6,7},{7,5},{5,3},{3,1},{1,0},{8,10},{10,12},{12... | collective-permute-start | bytes 2359304 | tf_op jit(solution)/shard_map/ppermute | solution.py:185
  172.8 14.7 %collective-permute-start.13 = (f32[2,32,3072]{2,1,0:T(8,128)S(1)}, f32[2,32,3072]{2,1,0:T(8,128)S(1)}, u32[]{:S(2)}, u32[]{:S(2)}) collective-permute-start(f32[2,32,3072]{2,1,0:T(8,128)S(1)} %collective-permute-done.11), channel_id=1, source_target_pairs={{2,0},{4,2},{6,4},{7,6},{5,7},{3,5},{1,3},{0,1},{10,8},{12,10},{14... | collective-permute-start | bytes 2359304 | tf_op jit(solution)/shard_map/ppermute | solution.py:186
  215.8 40.7 %copy-start.4 = (f32[128,128]{1,0:T(8,128)S(1)}, f32[128,128]{1,0:T(8,128)}, u32[]{:S(2)}) copy-start(f32[128,128]{1,0:T(8,128)} %fusion.56) | copy-start | bytes 196612
  257.5 41.4 %copy-start.3 = (f32[128,128]{1,0:T(8,128)S(1)}, f32[128,128]{1,0:T(8,128)}, u32[]{:S(2)}) copy-start(f32[128,128]{1,0:T(8,128)} %fusion.58) | copy-start | bytes 196612
  274.3 21.0 %all-to-all-start = ((f32[2,32,2048]{2,0,1:T(2,128)}), f32[2,32,2048]{2,0,1:T(2,128)S(1)}, u32[]{:S(2)}, u32[]{:S(2)}) async-start(f32[2,32,2048]{2,0,1:T(2,128)} %copy.145), calls=%async_computation.1 | async-start | bytes 1048576 | tf_op jit(solution)/shard_map/all_to_all | solution.py:164
  (1 other events, 5.0 us)
Sparse Core Ops, SparseCore 0:
  222.8 31.4 reduce-scatter.1

commit v2 on v1

--- a/solution.py
+++ b/solution.py
@@ -24,9 +24,9 @@
 
 def perm_matrix(new_pos, nbits):
     old = jnp.arange(2**nbits, dtype=jnp.int32)
-    moved = jnp.zeros_like(old)
-    for bit_num in range(nbits):
-        moved = moved + jnp.left_shift(jnp.right_shift(old, bit_num) & 1, new_pos[bit_num])
+    bits = jnp.right_shift(old[:, None], jnp.arange(nbits, dtype=jnp.int32)[None, :]) & 1
+    weights = jnp.left_shift(jnp.int32(1), new_pos)
+    moved = jnp.sum(bits * weights[None, :], axis=1)
     moved = lax.optimization_barrier(moved)
     return (old[:, None] == moved[None, :]).astype(jnp.float32)
 

time: 324 us -> 280 us (0.86); the launches traced: 330 us -> 281 us
  other arithmetic: 51 us -> 11.7 us
  local copies, waits for them, and re-layouts: 56.1 us -> 41.8 us
  waiting for transfers between devices: 113 us -> 117 us
    add x8 -> x0, other arithmetic: 40.1 us -> none  [perm_matrix(): moved + jnp.left_shift(jnp.right_shift(old, bit_num) & 1, new_pos[bit_num])]
    slice x8 -> x0, local copies, waits for them, and re-layouts: 5.49 us -> none  [perm_matrix(): new_pos[bit_num]]
    ppermute x7, waiting for transfers between devices: 61.8 us -> 66.1 us  [ring_all_gather(): ahead = lax.ppermute(ahead, axis, fwd)]
    transpose x2, local copies, waits for them, and re-layouts: 12 us -> 8.19 us  [run(): x = jnp.transpose(x, (0, 1, 3, 2, 4))]
  transfers between devices with their start and end apart: 16 -> 16, of which waited for: 10 -> 10; matrix products, arithmetic and copies ran while one was open for 23% -> 11% of each run, Pallas kernels for 0% -> 0%
where the time goes in v2:
time: 280 us; the launch traced here: 281 us
  waiting for transfers between devices  117 us (42%)
  matrix products  49.9 us (18%)
  local copies, waits for them, and re-layouts  41.8 us (15%)
  between operations  34.5 us (12%)
  starting transfers between devices  21.6 us (8%)
  other arithmetic  11.7 us (4%)
  loops' own time  3.8 us (1%)
    ppermute x7, waiting for transfers between devices, ring_all_gather(): ahead = lax.ppermute(ahead, axis, fwd)  66.1 us
    dot_general x4, matrix products, cross_dot(): lax.dot_general(left, right, (((1,), (1,)), ((), ())), precision=lax.Prec...  33.6 us
    reduce_scatter x1, waiting for transfers between devices, per_device(): lax.psum_scatter(partial_sums, 'bond', scatter_dimension=2, tiled=True)  31.1 us
    all_to_all x1, waiting for transfers between devices, regroup(): lax.all_to_all(block, ('bond', 'rows'), split_axis=1, concat_axis=1, tile...  15.6 us
    ppermute x7, starting transfers between devices, ring_all_gather(): ahead = lax.ppermute(ahead, axis, fwd)  13.8 us
    dot_general x4, matrix products, permute_rows(): jnp.einsum('no,pol->pnl', mat, block, precision=lax.Precision.HIGHEST)  11.5 us
    transpose x2, local copies, waits for them, and re-layouts, run(): x = jnp.transpose(x, (0, 1, 3, 2, 4))  8.19 us
    reshape x3, local copies, waits for them, and re-layouts, run(): return x.reshape(planes, 2 ** rbits, 2 ** cbits)  5.73 us
  transfers between devices with their start and end apart: 16, of which 10 were waited for; matrix products, arithmetic and copies ran while one was open for 11% of the time, Pallas kernels for 0%

profile of v2, /device:TPU:0, one launch (start us, length us, event | category | flops | bytes accessed | tf_op | source)
XLA Modules:
  0.0 280.6 jit_solution(18038914303933868484)
XLA Ops:
  6.6 2.5 fusion.89
  9.1 3.1 %collective-permute-start = (f32[2,32,3072]{2,1,0:T(8,128)}, f32[2,32,3072]{2,1,0:T(8,128)}, u32[]{:S(2)}, u32[]{:S(2)}) collective-permute-start(f32[2,32,3072]{2,1,0:T(8,128)} %get-tuple-element.70), channel_id=1, source_target_pairs={{0,2},{2,4},{4,6},{6,7},{7,5},{5,3},{3,1},{1,0},{8,10},{10,12},{12... | collective-permute-start | bytes 2359304 | tf_op jit(solution)/shard_map/ppermute | solution.py:185
  35.4 15.9 %collective-permute-done.2 = f32[2,32,3072]{2,1,0:T(8,128)} collective-permute-done((f32[2,32,3072]{2,1,0:T(8,128)}, f32[2,32,3072]{2,1,0:T(8,128)}, u32[]{:S(2)}, u32[]{:S(2)}) %collective-permute-start.2) | collective-permute-done | bytes 786464 | tf_op jit(solution)/shard_map/ppermute | solution.py:185
  80.4 13.1 %collective-permute-done.6 = f32[2,32,3072]{2,1,0:T(8,128)S(1)} collective-permute-done((f32[2,32,3072]{2,1,0:T(8,128)}, f32[2,32,3072]{2,1,0:T(8,128)S(1)}, u32[]{:S(2)}, u32[]{:S(2)}) %collective-permute-start.6) | collective-permute-done | bytes 786464 | tf_op jit(solution)/shard_map/ppermute | solution.py:185
  99.5 11.8 %collective-permute-done.8 = f32[2,32,3072]{2,1,0:T(8,128)S(1)} collective-permute-done((f32[2,32,3072]{2,1,0:T(8,128)S(1)}, f32[2,32,3072]{2,1,0:T(8,128)S(1)}, u32[]{:S(2)}, u32[]{:S(2)}) %collective-permute-start.8) | collective-permute-done | bytes 786464 | tf_op jit(solution)/shard_map/ppermute | solution.py:185
  114.9 14.0 %collective-permute-done.10 = f32[2,32,3072]{2,1,0:T(8,128)S(1)} collective-permute-done((f32[2,32,3072]{2,1,0:T(8,128)S(1)}, f32[2,32,3072]{2,1,0:T(8,128)S(1)}, u32[]{:S(2)}, u32[]{:S(2)}) %collective-permute-start.10) | collective-permute-done | bytes 786464 | tf_op jit(solution)/shard_map/ppermute | solution.py:185
  132.6 11.3 %collective-permute-done.12 = f32[2,32,3072]{2,1,0:T(8,128)S(1)} collective-permute-done((f32[2,32,3072]{2,1,0:T(8,128)S(1)}, f32[2,32,3072]{2,1,0:T(8,128)S(1)}, u32[]{:S(2)}, u32[]{:S(2)}) %collective-permute-start.12) | collective-permute-done | bytes 786464 | tf_op jit(solution)/shard_map/ppermute | solution.py:185
  144.0 2.4 collective-permute-done.13
  146.5 5.3 %fusion.2 = f32[512,512]{1,0:T(8,128)S(1)} fusion(f32[2,512,3072]{2,1,0:T(8,128)S(1)} %bitcast.202, f32[2,512,3072]{2,1,0:T(8,128)S(1)} %constant_dynamic-update-slice_fusion), kind=kOutput, calls=%fused_computation.17 | convolution fusion | flops 4831838208 | bytes 13631488 | tf_op jit(solution)/shard_map/dot_general | solution.py:11
  151.8 5.3 %fusion = f32[512,512]{1,0:T(8,128)S(1)} fusion(f32[2,512,3072]{2,1,0:T(8,128)S(1)} %bitcast.202, f32[2,512,3072]{2,1,0:T(8,128)S(1)} %constant_dynamic-update-slice_fusion), kind=kOutput, calls=%fused_computation.15 | convolution fusion | flops 4831838208 | bytes 13631488 | tf_op jit(solution)/shard_map/dot_general | solution.py:11
  157.2 17.5 %fusion.25 = f32[1,512,512]{1,2,0:T(8,128)S(1)} fusion(f32[512,512]{1,0:T(8,128)S(1)} %fusion.2, f32[2,512,3072]{2,1,0:T(8,128)S(1)} %bitcast.202, f32[2,512,3072]{2,1,0:T(8,128)S(1)} %constant_dynamic-update-slice_fusion), kind=kOutput, calls=%fused_computation.37 | convolution fusion | flops 4832100352 | bytes 14680064 | tf_op jit(solution)/shard_map/dot_general | solution.py:11
  174.7 5.3 %fusion.35 = f32[1,512,512]{1,2,0:T(8,128)S(1)} fusion(f32[512,512]{1,0:T(8,128)S(1)} %fusion, f32[2,512,3072]{2,1,0:T(8,128)S(1)} %bitcast.202, f32[2,512,3072]{2,1,0:T(8,128)S(1)} %constant_dynamic-update-slice_fusion), kind=kOutput, calls=%fused_computation.39 | convolution fusion | flops 4832100352 | bytes 14680064 | tf_op jit(solution)/shard_map/dot_general | solution.py:11
  182.2 31.1 %reduce-scatter.2.cloned.1.call-done = f32[2,512,128]{1,2,0:T(8,128)} async-done(((f32[2,512,512]{1,2,0:T(8,128)}), f32[2,512,128]{1,2,0:T(8,128)}) %reduce-scatter.2.cloned.1.call-update) | async-done | bytes 524304 | tf_op jit(solution)/shard_map/reduce_scatter | solution.py:201
  216.4 11.4 %conditional.2 = (f32[2,512,128]{2,1,0:T(8,128)S(1)}) conditional(s32[]{:T(128)} %clamp.7, f32[2,512,128]{2,1,0:T(8,128)S(1)} %fusion.54, f32[2,512,128]{2,1,0:T(8,128)S(1)} %fusion.54, f32[2,512,128]{2,1,0:T(8,128)S(1)} %fusion.54, f32[2,512,128]{2,1,0:T(8,128)S(1)} %fusion.54, ...), branch_computations={%region_31.32_spmd, %region_32.33_spmd, %region_33.34_spmd, %regio... | conditional | bytes 5242888 | solution.py:52
  216.4 2.5 reshape.273
  219.0 5.2 %copy.121 = f32[2,64,8,8,16]{4,3,2,1,0:T(8,128)} copy(f32[2,64,8,8,16]{4,2,3,1,0:T(8,128)} %bitcast.209) | data formatting | bytes 1048576 | tf_op jit(solution)/shard_map/cond/branch_3_fun/transpose | solution.py:47
  224.2 3.2 %reshape.274 = f32[2,512,128]{2,1,0:T(8,128)S(1)} reshape(f32[2,64,8,8,16]{4,3,2,1,0:T(8,128)} %copy.121) | data formatting | bytes 1048576 | tf_op jit(solution)/shard_map/cond/branch_3_fun/reshape | solution.py:48
  227.8 3.1 %convolution_bitcast_fusion.2 = f32[2,512,128]{1,2,0:T(8,128)S(1)} fusion(f32[2,512,128]{2,1,0:T(8,128)S(1)} %get-tuple-element.108, f32[512,512]{1,0:T(8,128)} %fusion.45), kind=kOutput, calls=%fused_computation.42 | convolution fusion | flops 805306368 | bytes 2097152 | tf_op jit(solution)/shard_map/no,pol->pnl/dot_general | solution.py:35
  233.3 4.8 %all-to-all-start = ((f32[2,32,2048]{2,0,1:T(2,128)}), f32[2,32,2048]{2,0,1:T(2,128)S(1)}, u32[]{:S(2)}, u32[]{:S(2)}) async-start(f32[2,32,2048]{2,0,1:T(2,128)} %copy.145), calls=%async_computation.1 | async-start | bytes 1048576 | tf_op jit(solution)/shard_map/all_to_all | solution.py:164
  238.7 15.6 %all-to-all-done = f32[2,32,2048]{2,0,1:T(2,128)S(1)} async-done(((f32[2,32,2048]{2,0,1:T(2,128)}), f32[2,32,2048]{2,0,1:T(2,128)S(1)}, u32[]{:S(2)}, u32[]{:S(2)}) %all-to-all-start) | async-done | bytes 524320 | tf_op jit(solution)/shard_map/all_to_all | solution.py:164
  254.7 3.1 %convolution_bitcast_fusion.1 = f32[2,512,128]{1,2,0:T(8,128)S(1)} fusion(f32[2,512,128]{2,1,0:T(8,128)S(1)} %reshape.300, f32[512,512]{1,0:T(8,128)} %fusion.46), kind=kOutput, calls=%fused_computation.41 | convolution fusion | flops 805306368 | bytes 2097152 | tf_op jit(solution)/shard_map/no,pol->pnl/dot_general | solution.py:35
  258.8 9.6 %conditional.3 = (f32[2,512,128]{2,1,0:T(8,128)S(1)}) conditional(s32[]{:T(128)} %clamp.6, f32[2,512,128]{2,1,0:T(8,128)S(1)} %fusion.50, f32[2,512,128]{2,1,0:T(8,128)S(1)} %fusion.50, f32[2,512,128]{2,1,0:T(8,128)S(1)} %fusion.50, f32[2,512,128]{2,1,0:T(8,128)S(1)} %fusion.50, ...), branch_computations={%region_39.40_spmd, %region_40.41_spmd, %region_41.42_spmd, %regio... | conditional | bytes 5242888 | solution.py:52
  259.8 3.0 %copy.134 = f32[2,16,32,32,4]{2,1,4,3,0:T(8,128)} copy(f32[2,16,32,32,4]{3,1,4,2,0:T(8,128)S(1)} %bitcast.212) | data formatting | bytes 1048576 | tf_op jit(solution)/shard_map/cond/branch_5_fun/transpose | solution.py:47
  268.4 3.2 %convolution_bitcast_fusion = f32[2,512,128]{1,2,0:T(8,128)S(1)} fusion(f32[2,512,128]{2,1,0:T(8,128)S(1)} %get-tuple-element.109, f32[512,512]{1,0:T(8,128)} %fusion.47), kind=kOutput, calls=%fused_computation.40 | convolution fusion | flops 805306368 | bytes 2097152 | tf_op jit(solution)/shard_map/no,pol->pnl/dot_general | solution.py:35
  (143 shorter events, 59.8 us)
Async XLA Ops:
  6.5 48.1 %copy-start.6 = (s32[8]{0:T(128)S(1)}, s32[8]{0:T(128)}, u32[]{:S(2)}) copy-start(s32[8]{0:T(128)} %constant.204.clone) | copy-start | bytes 100
  6.5 57.8 %copy-start.5 = (s32[8]{0:T(128)S(1)}, s32[8]{0:T(128)}, u32[]{:S(2)}) copy-start(s32[8]{0:T(128)} %constant.205.clone) | copy-start | bytes 100
  6.5 68.8 %copy-start.2 = (f32[2,64,3072]{2,1,0:T(8,128)S(1)}, f32[2,64,3072]{2,1,0:T(8,128)}, u32[]{:S(2)}) copy-start(f32[2,64,3072]{2,1,0:T(8,128)} %param.27) | copy-start | bytes 4718596
  6.5 206.7 %reduce-scatter.2.cloned.1.call-start = ((), (), s32[]{:S(2)}) async-start(), calls=%async_computation.2 | async-start | bytes 2621440 | tf_op jit(solution)/shard_map/reduce_scatter | solution.py:201
  9.1 22.9 %collective-permute-start = (f32[2,32,3072]{2,1,0:T(8,128)}, f32[2,32,3072]{2,1,0:T(8,128)}, u32[]{:S(2)}, u32[]{:S(2)}) collective-permute-start(f32[2,32,3072]{2,1,0:T(8,128)} %get-tuple-element.70), channel_id=1, source_target_pairs={{0,2},{2,4},{4,6},{6,7},{7,5},{5,3},{3,1},{1,0},{8,10},{10,12},{12... | collective-permute-start | bytes 2359304 | tf_op jit(solution)/shard_map/ppermute | solution.py:185
  12.1 21.9 %collective-permute-start.1 = (f32[2,32,3072]{2,1,0:T(8,128)S(1)}, f32[2,32,3072]{2,1,0:T(8,128)S(1)}, u32[]{:S(2)}, u32[]{:S(2)}) collective-permute-start(f32[2,32,3072]{2,1,0:T(8,128)S(1)} %get-tuple-element.69), channel_id=1, source_target_pairs={{2,0},{4,2},{6,4},{7,6},{5,7},{3,5},{1,3},{0,1},{10,8},{12,10},{14... | collective-permute-start | bytes 2359304 | tf_op jit(solution)/shard_map/ppermute | solution.py:186
  32.0 19.3 %collective-permute-start.2 = (f32[2,32,3072]{2,1,0:T(8,128)}, f32[2,32,3072]{2,1,0:T(8,128)}, u32[]{:S(2)}, u32[]{:S(2)}) collective-permute-start(f32[2,32,3072]{2,1,0:T(8,128)} %collective-permute-done), channel_id=1, source_target_pairs={{0,2},{2,4},{4,6},{6,7},{7,5},{5,3},{3,1},{1,0},{8,10},{10,12},{12... | collective-permute-start | bytes 2359304 | tf_op jit(solution)/shard_map/ppermute | solution.py:185
  34.0 19.7 %collective-permute-start.3 = (f32[2,32,3072]{2,1,0:T(8,128)S(1)}, f32[2,32,3072]{2,1,0:T(8,128)}, u32[]{:S(2)}, u32[]{:S(2)}) collective-permute-start(f32[2,32,3072]{2,1,0:T(8,128)S(1)} %collective-permute-done.1), channel_id=1, source_target_pairs={{2,0},{4,2},{6,4},{7,6},{5,7},{3,5},{1,3},{0,1},{10,8},{12,10},{14... | collective-permute-start | bytes 2359304 | tf_op jit(solution)/shard_map/ppermute | solution.py:186
  51.3 24.2 %collective-permute-start.4 = (f32[2,32,3072]{2,1,0:T(8,128)}, f32[2,32,3072]{2,1,0:T(8,128)}, u32[]{:S(2)}, u32[]{:S(2)}) collective-permute-start(f32[2,32,3072]{2,1,0:T(8,128)} %collective-permute-done.2), channel_id=1, source_target_pairs={{0,2},{2,4},{4,6},{6,7},{7,5},{5,3},{3,1},{1,0},{8,10},{10,12},{12... | collective-permute-start | bytes 2359304 | tf_op jit(solution)/shard_map/ppermute | solution.py:185
  53.7 24.9 %collective-permute-start.5 = (f32[2,32,3072]{2,1,0:T(8,128)}, f32[2,32,3072]{2,1,0:T(8,128)}, u32[]{:S(2)}, u32[]{:S(2)}) collective-permute-start(f32[2,32,3072]{2,1,0:T(8,128)} %collective-permute-done.3), channel_id=1, source_target_pairs={{2,0},{4,2},{6,4},{7,6},{5,7},{3,5},{1,3},{0,1},{10,8},{12,10},{14... | collective-permute-start | bytes 2359304 | tf_op jit(solution)/shard_map/ppermute | solution.py:186
  75.4 71.1 %slice-start = ((s8[12582912]{0:T(1024)(128)(4,1)}), s8[4194304]{0:T(1024)(128)(4,1)S(1)}, s32[]{:S(2)}) async-start(s8[12582912]{0:T(1024)(128)(4,1)} %bitcast.201), calls=%async_computation.3 | async-start | bytes 8388608
  75.6 18.0 %collective-permute-start.6 = (f32[2,32,3072]{2,1,0:T(8,128)}, f32[2,32,3072]{2,1,0:T(8,128)S(1)}, u32[]{:S(2)}, u32[]{:S(2)}) collective-permute-start(f32[2,32,3072]{2,1,0:T(8,128)} %collective-permute-done.4), channel_id=1, source_target_pairs={{0,2},{2,4},{4,6},{6,7},{7,5},{5,3},{3,1},{1,0},{8,10},{10,12},{12... | collective-permute-start | bytes 2359304 | tf_op jit(solution)/shard_map/ppermute | solution.py:185
  78.5 17.9 %collective-permute-start.7 = (f32[2,32,3072]{2,1,0:T(8,128)}, f32[2,32,3072]{2,1,0:T(8,128)S(1)}, u32[]{:S(2)}, u32[]{:S(2)}) collective-permute-start(f32[2,32,3072]{2,1,0:T(8,128)} %collective-permute-done.5), channel_id=1, source_target_pairs={{2,0},{4,2},{6,4},{7,6},{5,7},{3,5},{1,3},{0,1},{10,8},{12,10},{14... | collective-permute-start | bytes 2359304 | tf_op jit(solution)/shard_map/ppermute | solution.py:186
  80.4 66.0 %slice-start.1 = ((s8[12582912]{0:T(1024)(128)(4,1)}), s8[4194304]{0:T(1024)(128)(4,1)S(1)}, s32[]{:S(2)}) async-start(s8[12582912]{0:T(1024)(128)(4,1)} %bitcast.201), calls=%async_computation.4 | async-start | bytes 8388608
  93.5 17.7 %collective-permute-start.8 = (f32[2,32,3072]{2,1,0:T(8,128)S(1)}, f32[2,32,3072]{2,1,0:T(8,128)S(1)}, u32[]{:S(2)}, u32[]{:S(2)}) collective-permute-start(f32[2,32,3072]{2,1,0:T(8,128)S(1)} %collective-permute-done.6), channel_id=1, source_target_pairs={{0,2},{2,4},{4,6},{6,7},{7,5},{5,3},{3,1},{1,0},{8,10},{10,12},{12... | collective-permute-start | bytes 2359304 | tf_op jit(solution)/shard_map/ppermute | solution.py:185
  96.5 17.8 %collective-permute-start.9 = (f32[2,32,3072]{2,1,0:T(8,128)S(1)}, f32[2,32,3072]{2,1,0:T(8,128)S(1)}, u32[]{:S(2)}, u32[]{:S(2)}) collective-permute-start(f32[2,32,3072]{2,1,0:T(8,128)S(1)} %collective-permute-done.7), channel_id=1, source_target_pairs={{2,0},{4,2},{6,4},{7,6},{5,7},{3,5},{1,3},{0,1},{10,8},{12,10},{14... | collective-permute-start | bytes 2359304 | tf_op jit(solution)/shard_map/ppermute | solution.py:186
  111.2 17.7 %collective-permute-start.10 = (f32[2,32,3072]{2,1,0:T(8,128)S(1)}, f32[2,32,3072]{2,1,0:T(8,128)S(1)}, u32[]{:S(2)}, u32[]{:S(2)}) collective-permute-start(f32[2,32,3072]{2,1,0:T(8,128)S(1)} %collective-permute-done.8), channel_id=1, source_target_pairs={{0,2},{2,4},{4,6},{6,7},{7,5},{5,3},{3,1},{1,0},{8,10},{10,12},{12... | collective-permute-start | bytes 2359304 | tf_op jit(solution)/shard_map/ppermute | solution.py:185
  114.2 17.5 %collective-permute-start.11 = (f32[2,32,3072]{2,1,0:T(8,128)S(1)}, f32[2,32,3072]{2,1,0:T(8,128)S(1)}, u32[]{:S(2)}, u32[]{:S(2)}) collective-permute-start(f32[2,32,3072]{2,1,0:T(8,128)S(1)} %collective-permute-done.9), channel_id=1, source_target_pairs={{2,0},{4,2},{6,4},{7,6},{5,7},{3,5},{1,3},{0,1},{10,8},{12,10},{14... | collective-permute-start | bytes 2359304 | tf_op jit(solution)/shard_map/ppermute | solution.py:186
  114.9 31.6 %slice-start.2 = ((s8[12582912]{0:T(1024)(128)(4,1)}), s8[4194304]{0:T(1024)(128)(4,1)S(1)}, s32[]{:S(2)}) async-start(s8[12582912]{0:T(1024)(128)(4,1)} %bitcast.201), calls=%async_computation.5 | async-start | bytes 8388608
  128.9 15.0 %collective-permute-start.12 = (f32[2,32,3072]{2,1,0:T(8,128)S(1)}, f32[2,32,3072]{2,1,0:T(8,128)S(1)}, u32[]{:S(2)}, u32[]{:S(2)}) collective-permute-start(f32[2,32,3072]{2,1,0:T(8,128)S(1)} %collective-permute-done.10), channel_id=1, source_target_pairs={{0,2},{2,4},{4,6},{6,7},{7,5},{5,3},{3,1},{1,0},{8,10},{10,12},{12... | collective-permute-start | bytes 2359304 | tf_op jit(solution)/shard_map/ppermute | solution.py:185
  131.7 14.7 %collective-permute-start.13 = (f32[2,32,3072]{2,1,0:T(8,128)S(1)}, f32[2,32,3072]{2,1,0:T(8,128)S(1)}, u32[]{:S(2)}, u32[]{:S(2)}) collective-permute-start(f32[2,32,3072]{2,1,0:T(8,128)S(1)} %collective-permute-done.11), channel_id=1, source_target_pairs={{2,0},{4,2},{6,4},{7,6},{5,7},{3,5},{1,3},{0,1},{10,8},{12,10},{14... | collective-permute-start | bytes 2359304 | tf_op jit(solution)/shard_map/ppermute | solution.py:186
  174.7 40.7 %copy-start.4 = (f32[128,128]{1,0:T(8,128)S(1)}, f32[128,128]{1,0:T(8,128)}, u32[]{:S(2)}) copy-start(f32[128,128]{1,0:T(8,128)} %fusion.56) | copy-start | bytes 196612
  216.4 41.4 %copy-start.3 = (f32[128,128]{1,0:T(8,128)S(1)}, f32[128,128]{1,0:T(8,128)}, u32[]{:S(2)}) copy-start(f32[128,128]{1,0:T(8,128)} %fusion.58) | copy-start | bytes 196612
  233.3 21.0 %all-to-all-start = ((f32[2,32,2048]{2,0,1:T(2,128)}), f32[2,32,2048]{2,0,1:T(2,128)S(1)}, u32[]{:S(2)}, u32[]{:S(2)}) async-start(f32[2,32,2048]{2,0,1:T(2,128)} %copy.145), calls=%async_computation.1 | async-start | bytes 1048576 | tf_op jit(solution)/shard_map/all_to_all | solution.py:164
  (2 other events, 11.3 us)
Sparse Core Ops, SparseCore 0:
  181.8 31.4 reduce-scatter.1

commit v3 on v2

--- a/solution.py
+++ b/solution.py
@@ -107,17 +107,12 @@
     total_bits = ROW_BITS + COL_BITS
     lrows = ROW_BITS - row_devbits
     lcols = COL_BITS - bond_devbits
+    prows = lrows - bond_devbits
     nlocal = lrows + lcols
     devbits = row_devbits + bond_devbits
-    local_of = []
-    for bit in range(total_bits):
-        if bit < lcols:
-            local_of.append(bit)
-        elif COL_BITS <= bit < COL_BITS + lrows:
-            local_of.append(bit - COL_BITS + lcols)
-        else:
-            local_of.append(-1)
-    local_of = jnp.array(local_of, dtype=jnp.int32)
+    local_of = jnp.array(
+        [bit if bit < nlocal else -1 for bit in range(total_bits)], dtype=jnp.int32
+    )
     out_dev = [COL_BITS + lrows + k for k in range(row_devbits)] + [
         lcols + k for k in range(bond_devbits)
     ]
@@ -126,26 +121,16 @@
     is_dev = jnp.any(pos[:, None] == dev_src[None, :], axis=1)
     keep = ~is_dev
     keep_rank = rank_within(pos, keep)
-    src_a = jnp.zeros((nlocal,), jnp.int32).at[
-        jnp.where(keep, keep_rank, nlocal)
-    ].set(pos, mode="drop")
-    src_a = src_a.at[nlocal - devbits + jnp.arange(devbits)].set(dev_src)
-    plan_a = plan_permute(src_a, lrows, lcols)
-    src_dev_bits = [COL_BITS + lrows + k for k in range(row_devbits)] + [
-        lcols + k for k in range(bond_devbits)
-    ]
-    pos_w = jnp.full((total_bits,), -1, jnp.int32)
     within = jnp.zeros((nlocal,), jnp.int32).at[jnp.where(keep, keep_rank, nlocal)].set(
         pos, mode="drop"
     )
-    prod_of_local = jnp.array(
-        [b for b in range(total_bits) if b < lcols]
-        + [b for b in range(COL_BITS, COL_BITS + lrows)],
-        dtype=jnp.int32,
-    )
-    pos_w = pos_w.at[prod_of_local[within[: nlocal - devbits]]].set(
-        jnp.arange(nlocal - devbits, dtype=jnp.int32)
-    )
+    src_a = within.at[nlocal - devbits + jnp.arange(devbits)].set(dev_src)
+    plan_a = plan_permute(src_a, prows, COL_BITS)
+    src_dev_bits = [COL_BITS + lrows + k for k in range(row_devbits)] + [
+        COL_BITS + prows + k for k in range(bond_devbits)
+    ]
+    pos_w = jnp.full((total_bits,), -1, jnp.int32)
+    pos_w = pos_w.at[within[: nlocal - devbits]].set(jnp.arange(nlocal - devbits, dtype=jnp.int32))
     pos_w = pos_w.at[jnp.array(src_dev_bits, dtype=jnp.int32)].set(
         nlocal - devbits + jnp.arange(devbits, dtype=jnp.int32)
     )
@@ -157,12 +142,15 @@
 
 def regroup(block, plans):
     plan_a, plan_c = plans
-    planes, nrow, ncol = block.shape
-    devices = lax.axis_size("rows") * lax.axis_size("bond")
+    planes = block.shape[0]
+    nrows = lax.axis_size("rows")
+    nbond = lax.axis_size("bond")
+    lrows = 2**ROW_BITS // nrows
+    lcols = 2**COL_BITS // nbond
     block = apply_permute(block, plan_a)
-    block = block.reshape(planes, devices, -1)
+    block = block.reshape(planes, nrows * nbond, -1)
     block = lax.all_to_all(block, ("bond", "rows"), split_axis=1, concat_axis=1, tiled=True)
-    block = block.reshape(planes, nrow, ncol)
+    block = block.reshape(planes, lrows, lcols)
     return apply_permute(block, plan_c)
 
 
@@ -198,7 +186,7 @@
     real_part = cross_dot(amps_left[0], gathered[0]) - cross_dot(amps_left[1], gathered[1])
     imag_part = cross_dot(amps_left[0], gathered[1]) + cross_dot(amps_left[1], gathered[0])
     partial_sums = jnp.stack([real_part, imag_part])
-    block = lax.psum_scatter(partial_sums, "bond", scatter_dimension=2, tiled=True)
+    block = lax.psum_scatter(partial_sums, "bond", scatter_dimension=1, tiled=True)
     return regroup(block, plans)
 
 

time: 280 us -> 276 us (0.986); the launches traced: 281 us -> 272 us
  matrix products: 49.9 us -> 38.6 us
  local copies, waits for them, and re-layouts: 41.8 us -> 44.7 us
    dot_general x4, matrix products: 33.6 us -> 21.8 us  [cross_dot(): lax.dot_general(left, right, (((1,), (1,)), ((), ())), precision=lax.Prec...]
    reshape x2 -> x3, local copies, waits for them, and re-layouts: 3.08 us -> 6.91 us  [run(): x = x.reshape(planes, 2 ** (rbits - k), 2 ** k, 2 ** k, 2 ** (cbits - k))]
    dot_general x4, matrix products: 4.77 us -> 7.86 us  [permute_lanes(): jnp.einsum('no,pro->prn', mat, block, precision=lax.Precision.HIGHEST)]
    transpose x2 -> x1, local copies, waits for them, and re-layouts: 8.19 us -> 6.81 us  [run(): x = jnp.transpose(x, (0, 1, 3, 2, 4))]
where the time goes in v3:
time: 276 us; the launch traced here: 272 us
  waiting for transfers between devices  117 us (42%)
  local copies, waits for them, and re-layouts  44.7 us (16%)
  matrix products  38.6 us (14%)
  between operations  34.7 us (13%)
  starting transfers between devices  21.6 us (8%)
  other arithmetic  11.9 us (4%)
  loops' own time  3.66 us (1%)
    ppermute x7, waiting for transfers between devices, ring_all_gather(): ahead = lax.ppermute(ahead, axis, fwd)  66.1 us
    reduce_scatter x1, waiting for transfers between devices, per_device(): lax.psum_scatter(partial_sums, 'bond', scatter_dimension=1, tiled=True)  31 us
    dot_general x4, matrix products, cross_dot(): lax.dot_general(left, right, (((1,), (1,)), ((), ())), precision=lax.Prec...  21.8 us
    all_to_all x1, waiting for transfers between devices, regroup(): lax.all_to_all(block, ('bond', 'rows'), split_axis=1, concat_axis=1, tile...  15.6 us
    ppermute x7, starting transfers between devices, ring_all_gather(): ahead = lax.ppermute(ahead, axis, fwd)  13.8 us
    dot_general x4, matrix products, permute_rows(): jnp.einsum('no,pol->pnl', mat, block, precision=lax.Precision.HIGHEST)  8.92 us
    dot_general x4, matrix products, permute_lanes(): jnp.einsum('no,pro->prn', mat, block, precision=lax.Precision.HIGHEST)  7.86 us
    reshape x3, local copies, waits for them, and re-layouts, run(): x = x.reshape(planes, 2 ** (rbits - k), 2 ** k, 2 ** k, 2 ** (cbits - k))  6.91 us
  transfers between devices with their start and end apart: 16, of which 10 were waited for; matrix products, arithmetic and copies ran while one was open for 11% of the time, Pallas kernels for 0%

profile of v3, /device:TPU:0, one launch (start us, length us, event | category | flops | bytes accessed | tf_op | source)
XLA Modules:
  0.0 272.3 jit_solution(16158158267424948049)
XLA Ops:
  6.5 2.5 fusion.85
  9.0 3.1 %collective-permute-start = (f32[2,32,3072]{2,1,0:T(8,128)}, f32[2,32,3072]{2,1,0:T(8,128)}, u32[]{:S(2)}, u32[]{:S(2)}) collective-permute-start(f32[2,32,3072]{2,1,0:T(8,128)} %get-tuple-element.74), channel_id=1, source_target_pairs={{0,2},{2,4},{4,6},{6,7},{7,5},{5,3},{3,1},{1,0},{8,10},{10,12},{12... | collective-permute-start | bytes 2359304 | tf_op jit(solution)/shard_map/ppermute | solution.py:173
  34.2 15.9 %collective-permute-done.2 = f32[2,32,3072]{2,1,0:T(8,128)} collective-permute-done((f32[2,32,3072]{2,1,0:T(8,128)}, f32[2,32,3072]{2,1,0:T(8,128)}, u32[]{:S(2)}, u32[]{:S(2)}) %collective-permute-start.2) | collective-permute-done | bytes 786464 | tf_op jit(solution)/shard_map/ppermute | solution.py:173
  80.9 13.1 %collective-permute-done.6 = f32[2,32,3072]{2,1,0:T(8,128)S(1)} collective-permute-done((f32[2,32,3072]{2,1,0:T(8,128)}, f32[2,32,3072]{2,1,0:T(8,128)S(1)}, u32[]{:S(2)}, u32[]{:S(2)}) %collective-permute-start.6) | collective-permute-done | bytes 786464 | tf_op jit(solution)/shard_map/ppermute | solution.py:173
  100.0 11.8 %collective-permute-done.8 = f32[2,32,3072]{2,1,0:T(8,128)S(1)} collective-permute-done((f32[2,32,3072]{2,1,0:T(8,128)S(1)}, f32[2,32,3072]{2,1,0:T(8,128)S(1)}, u32[]{:S(2)}, u32[]{:S(2)}) %collective-permute-start.8) | collective-permute-done | bytes 786464 | tf_op jit(solution)/shard_map/ppermute | solution.py:173
  115.4 14.0 %collective-permute-done.10 = f32[2,32,3072]{2,1,0:T(8,128)S(1)} collective-permute-done((f32[2,32,3072]{2,1,0:T(8,128)S(1)}, f32[2,32,3072]{2,1,0:T(8,128)S(1)}, u32[]{:S(2)}, u32[]{:S(2)}) %collective-permute-start.10) | collective-permute-done | bytes 786464 | tf_op jit(solution)/shard_map/ppermute | solution.py:173
  133.1 11.3 %collective-permute-done.12 = f32[2,32,3072]{2,1,0:T(8,128)S(1)} collective-permute-done((f32[2,32,3072]{2,1,0:T(8,128)S(1)}, f32[2,32,3072]{2,1,0:T(8,128)S(1)}, u32[]{:S(2)}, u32[]{:S(2)}) %collective-permute-start.12) | collective-permute-done | bytes 786464 | tf_op jit(solution)/shard_map/ppermute | solution.py:173
  144.5 2.4 collective-permute-done.13
  147.0 5.3 %fusion.2 = f32[512,512]{1,0:T(8,128)S(1)} fusion(f32[2,512,3072]{2,1,0:T(8,128)S(1)} %bitcast.198, f32[2,512,3072]{2,1,0:T(8,128)S(1)} %constant_dynamic-update-slice_fusion), kind=kOutput, calls=%fused_computation.20 | convolution fusion | flops 4831838208 | bytes 13631488 | tf_op jit(solution)/shard_map/dot_general | solution.py:11
  152.3 5.3 %fusion = f32[512,512]{1,0:T(8,128)S(1)} fusion(f32[2,512,3072]{2,1,0:T(8,128)S(1)} %bitcast.198, f32[2,512,3072]{2,1,0:T(8,128)S(1)} %constant_dynamic-update-slice_fusion), kind=kOutput, calls=%fused_computation.18 | convolution fusion | flops 4831838208 | bytes 13631488 | tf_op jit(solution)/shard_map/dot_general | solution.py:11
  157.7 5.8 %fusion.25 = f32[1,512,512]{1,2,0:T(8,128)S(1)} fusion(f32[512,512]{1,0:T(8,128)S(1)} %fusion.2, f32[2,512,3072]{2,1,0:T(8,128)S(1)} %bitcast.198, f32[2,512,3072]{2,1,0:T(8,128)S(1)} %constant_dynamic-update-slice_fusion), kind=kOutput, calls=%fused_computation.40 | convolution fusion | flops 4832100352 | bytes 14680064 | tf_op jit(solution)/shard_map/dot_general | solution.py:11
  163.5 5.3 %fusion.35 = f32[1,512,512]{1,2,0:T(8,128)S(1)} fusion(f32[512,512]{1,0:T(8,128)S(1)} %fusion, f32[2,512,3072]{2,1,0:T(8,128)S(1)} %bitcast.198, f32[2,512,3072]{2,1,0:T(8,128)S(1)} %constant_dynamic-update-slice_fusion), kind=kOutput, calls=%fused_computation.42 | convolution fusion | flops 4832100352 | bytes 14680064 | tf_op jit(solution)/shard_map/dot_general | solution.py:11
  171.0 31.0 %reduce-scatter.2.cloned.1.call-done = f32[2,128,512]{1,2,0:T(8,128)} async-done(((f32[2,512,512]{1,2,0:T(8,128)}), f32[2,128,512]{1,2,0:T(8,128)}) %reduce-scatter.2.cloned.1.call-update) | async-done | bytes 524304 | tf_op jit(solution)/shard_map/reduce_scatter | solution.py:189
  205.6 5.2 %conditional.2 = (f32[2,128,512]{2,1,0:T(8,128)S(1)}) conditional(s32[]{:T(128)} %clamp.7, f32[2,128,512]{2,1,0:T(8,128)S(1)} %fusion.44, f32[2,128,512]{2,1,0:T(8,128)S(1)} %fusion.44, f32[2,128,512]{2,1,0:T(8,128)S(1)} %fusion.44, f32[2,128,512]{2,1,0:T(8,128)S(1)} %fusion.44, ...), branch_computations={%region_31.32_spmd, %region_32.33_spmd, %region_33.34_spmd, %regio... | conditional | bytes 5242888 | solution.py:52
  207.7 2.3 copy.169
  211.8 3.2 %fusion.42 = f32[2,128,512]{2,1,0:T(8,128)S(1)} fusion(f32[2,128,512]{1,2,0:T(8,128)S(1)} %convolution_bitcast_fusion.2, f32[512,512]{1,0:T(8,128)} %fusion.47), kind=kOutput, calls=%fused_computation.49 | convolution fusion | flops 805306368 | bytes 2097152 | tf_op jit(solution)/shard_map/no,pro->prn/dot_general | solution.py:39
  216.4 4.8 %all-to-all-start = ((f32[2,32,2048]{2,0,1:T(2,128)}), f32[2,32,2048]{2,0,1:T(2,128)S(1)}, u32[]{:S(2)}, u32[]{:S(2)}) async-start(f32[2,32,2048]{2,0,1:T(2,128)} %copy.146), calls=%async_computation.1 | async-start | bytes 1048576 | tf_op jit(solution)/shard_map/all_to_all | solution.py:152
  221.9 15.6 %all-to-all-done = f32[2,32,2048]{2,0,1:T(2,128)S(1)} async-done(((f32[2,32,2048]{2,0,1:T(2,128)}), f32[2,32,2048]{2,0,1:T(2,128)S(1)}, u32[]{:S(2)}, u32[]{:S(2)}) %all-to-all-start) | async-done | bytes 524320 | tf_op jit(solution)/shard_map/all_to_all | solution.py:152
  237.8 3.1 %convolution_bitcast_fusion.1 = f32[2,512,128]{1,2,0:T(8,128)S(1)} fusion(f32[2,512,128]{2,1,0:T(8,128)S(1)} %reshape.287, f32[512,512]{1,0:T(8,128)} %fusion.48), kind=kOutput, calls=%fused_computation.44 | convolution fusion | flops 805306368 | bytes 2097152 | tf_op jit(solution)/shard_map/no,pol->pnl/dot_general | solution.py:35
  242.0 17.9 %conditional.3 = (f32[2,512,128]{2,1,0:T(8,128)S(1)}) conditional(s32[]{:T(128)} %clamp.6, f32[2,512,128]{2,1,0:T(8,128)S(1)} %fusion.52, f32[2,512,128]{2,1,0:T(8,128)S(1)} %fusion.52, f32[2,512,128]{2,1,0:T(8,128)S(1)} %fusion.52, f32[2,512,128]{2,1,0:T(8,128)S(1)} %fusion.52, ...), branch_computations={%region_39.40_spmd, %region_40.41_spmd, %region_41.42_spmd, %regio... | conditional | bytes 5242888 | solution.py:52
  242.5 2.8 %reshape.276 = f32[2,32,16,16,8]{2,1,4,3,0:T(8,128)} reshape(f32[2,512,128]{1,2,0:T(8,128)S(1)} %copy.150) | data formatting | bytes 1048576 | tf_op jit(solution)/shard_map/cond/branch_4_fun/reshape | solution.py:46
  245.3 6.8 %copy.133 = f32[2,32,16,16,8]{2,1,4,3,0:T(8,128)} copy(f32[2,32,16,16,8]{3,1,4,2,0:T(8,128)} %bitcast.201) | data formatting | bytes 1048576 | tf_op jit(solution)/shard_map/cond/branch_4_fun/transpose | solution.py:47
  252.1 4.5 %reshape.277 = f32[2,512,128]{1,2,0:T(8,128)S(1)} reshape(f32[2,32,16,16,8]{2,1,4,3,0:T(8,128)} %copy.133) | data formatting | bytes 1048576 | tf_op jit(solution)/shard_map/cond/branch_4_fun/reshape | solution.py:48
  259.9 3.2 %convolution_bitcast_fusion = f32[2,512,128]{1,2,0:T(8,128)S(1)} fusion(f32[2,512,128]{2,1,0:T(8,128)S(1)} %get-tuple-element.111, f32[512,512]{1,0:T(8,128)} %fusion.49), kind=kOutput, calls=%fused_computation.43 | convolution fusion | flops 805306368 | bytes 2097152 | tf_op jit(solution)/shard_map/no,pol->pnl/dot_general | solution.py:35
  (136 shorter events, 61.0 us)
Async XLA Ops:
  6.5 6.2 %copy-start = (s32[21]{0:T(128)S(1)}, s32[21]{0:T(128)}, u32[]{:S(2)}) copy-start(s32[21]{0:T(128)} %param.27) | copy-start | bytes 256
  6.5 69.3 %copy-start.2 = (f32[2,64,3072]{2,1,0:T(8,128)S(1)}, f32[2,64,3072]{2,1,0:T(8,128)}, u32[]{:S(2)}) copy-start(f32[2,64,3072]{2,1,0:T(8,128)} %param.26) | copy-start | bytes 4718596
  6.5 195.5 %reduce-scatter.2.cloned.1.call-start = ((), (), s32[]{:S(2)}) async-start(), calls=%async_computation.2 | async-start | bytes 2621440 | tf_op jit(solution)/shard_map/reduce_scatter | solution.py:189
  9.0 21.8 %collective-permute-start = (f32[2,32,3072]{2,1,0:T(8,128)}, f32[2,32,3072]{2,1,0:T(8,128)}, u32[]{:S(2)}, u32[]{:S(2)}) collective-permute-start(f32[2,32,3072]{2,1,0:T(8,128)} %get-tuple-element.74), channel_id=1, source_target_pairs={{0,2},{2,4},{4,6},{6,7},{7,5},{5,3},{3,1},{1,0},{8,10},{10,12},{12... | collective-permute-start | bytes 2359304 | tf_op jit(solution)/shard_map/ppermute | solution.py:173
  12.1 20.8 %collective-permute-start.1 = (f32[2,32,3072]{2,1,0:T(8,128)S(1)}, f32[2,32,3072]{2,1,0:T(8,128)S(1)}, u32[]{:S(2)}, u32[]{:S(2)}) collective-permute-start(f32[2,32,3072]{2,1,0:T(8,128)S(1)} %get-tuple-element.73), channel_id=1, source_target_pairs={{2,0},{4,2},{6,4},{7,6},{5,7},{3,5},{1,3},{0,1},{10,8},{12,10},{14... | collective-permute-start | bytes 2359304 | tf_op jit(solution)/shard_map/ppermute | solution.py:174
  30.9 19.3 %collective-permute-start.2 = (f32[2,32,3072]{2,1,0:T(8,128)}, f32[2,32,3072]{2,1,0:T(8,128)}, u32[]{:S(2)}, u32[]{:S(2)}) collective-permute-start(f32[2,32,3072]{2,1,0:T(8,128)} %collective-permute-done), channel_id=1, source_target_pairs={{0,2},{2,4},{4,6},{6,7},{7,5},{5,3},{3,1},{1,0},{8,10},{10,12},{12... | collective-permute-start | bytes 2359304 | tf_op jit(solution)/shard_map/ppermute | solution.py:173
  32.9 19.7 %collective-permute-start.3 = (f32[2,32,3072]{2,1,0:T(8,128)S(1)}, f32[2,32,3072]{2,1,0:T(8,128)}, u32[]{:S(2)}, u32[]{:S(2)}) collective-permute-start(f32[2,32,3072]{2,1,0:T(8,128)S(1)} %collective-permute-done.1), channel_id=1, source_target_pairs={{2,0},{4,2},{6,4},{7,6},{5,7},{3,5},{1,3},{0,1},{10,8},{12,10},{14... | collective-permute-start | bytes 2359304 | tf_op jit(solution)/shard_map/ppermute | solution.py:174
  50.2 25.8 %collective-permute-start.4 = (f32[2,32,3072]{2,1,0:T(8,128)}, f32[2,32,3072]{2,1,0:T(8,128)}, u32[]{:S(2)}, u32[]{:S(2)}) collective-permute-start(f32[2,32,3072]{2,1,0:T(8,128)} %collective-permute-done.2), channel_id=1, source_target_pairs={{0,2},{2,4},{4,6},{6,7},{7,5},{5,3},{3,1},{1,0},{8,10},{10,12},{12... | collective-permute-start | bytes 2359304 | tf_op jit(solution)/shard_map/ppermute | solution.py:173
  52.6 26.4 %collective-permute-start.5 = (f32[2,32,3072]{2,1,0:T(8,128)}, f32[2,32,3072]{2,1,0:T(8,128)}, u32[]{:S(2)}, u32[]{:S(2)}) collective-permute-start(f32[2,32,3072]{2,1,0:T(8,128)} %collective-permute-done.3), channel_id=1, source_target_pairs={{2,0},{4,2},{6,4},{7,6},{5,7},{3,5},{1,3},{0,1},{10,8},{12,10},{14... | collective-permute-start | bytes 2359304 | tf_op jit(solution)/shard_map/ppermute | solution.py:174
  75.8 71.1 %slice-start = ((s8[12582912]{0:T(1024)(128)(4,1)}), s8[4194304]{0:T(1024)(128)(4,1)S(1)}, s32[]{:S(2)}) async-start(s8[12582912]{0:T(1024)(128)(4,1)} %bitcast.197), calls=%async_computation.3 | async-start | bytes 8388608
  76.0 18.0 %collective-permute-start.6 = (f32[2,32,3072]{2,1,0:T(8,128)}, f32[2,32,3072]{2,1,0:T(8,128)S(1)}, u32[]{:S(2)}, u32[]{:S(2)}) collective-permute-start(f32[2,32,3072]{2,1,0:T(8,128)} %collective-permute-done.4), channel_id=1, source_target_pairs={{0,2},{2,4},{4,6},{6,7},{7,5},{5,3},{3,1},{1,0},{8,10},{10,12},{12... | collective-permute-start | bytes 2359304 | tf_op jit(solution)/shard_map/ppermute | solution.py:173
  79.0 17.9 %collective-permute-start.7 = (f32[2,32,3072]{2,1,0:T(8,128)}, f32[2,32,3072]{2,1,0:T(8,128)S(1)}, u32[]{:S(2)}, u32[]{:S(2)}) collective-permute-start(f32[2,32,3072]{2,1,0:T(8,128)} %collective-permute-done.5), channel_id=1, source_target_pairs={{2,0},{4,2},{6,4},{7,6},{5,7},{3,5},{1,3},{0,1},{10,8},{12,10},{14... | collective-permute-start | bytes 2359304 | tf_op jit(solution)/shard_map/ppermute | solution.py:174
  80.9 66.0 %slice-start.1 = ((s8[12582912]{0:T(1024)(128)(4,1)}), s8[4194304]{0:T(1024)(128)(4,1)S(1)}, s32[]{:S(2)}) async-start(s8[12582912]{0:T(1024)(128)(4,1)} %bitcast.197), calls=%async_computation.4 | async-start | bytes 8388608
  94.0 17.7 %collective-permute-start.8 = (f32[2,32,3072]{2,1,0:T(8,128)S(1)}, f32[2,32,3072]{2,1,0:T(8,128)S(1)}, u32[]{:S(2)}, u32[]{:S(2)}) collective-permute-start(f32[2,32,3072]{2,1,0:T(8,128)S(1)} %collective-permute-done.6), channel_id=1, source_target_pairs={{0,2},{2,4},{4,6},{6,7},{7,5},{5,3},{3,1},{1,0},{8,10},{10,12},{12... | collective-permute-start | bytes 2359304 | tf_op jit(solution)/shard_map/ppermute | solution.py:173
  96.9 17.8 %collective-permute-start.9 = (f32[2,32,3072]{2,1,0:T(8,128)S(1)}, f32[2,32,3072]{2,1,0:T(8,128)S(1)}, u32[]{:S(2)}, u32[]{:S(2)}) collective-permute-start(f32[2,32,3072]{2,1,0:T(8,128)S(1)} %collective-permute-done.7), channel_id=1, source_target_pairs={{2,0},{4,2},{6,4},{7,6},{5,7},{3,5},{1,3},{0,1},{10,8},{12,10},{14... | collective-permute-start | bytes 2359304 | tf_op jit(solution)/shard_map/ppermute | solution.py:174
  111.7 17.7 %collective-permute-start.10 = (f32[2,32,3072]{2,1,0:T(8,128)S(1)}, f32[2,32,3072]{2,1,0:T(8,128)S(1)}, u32[]{:S(2)}, u32[]{:S(2)}) collective-permute-start(f32[2,32,3072]{2,1,0:T(8,128)S(1)} %collective-permute-done.8), channel_id=1, source_target_pairs={{0,2},{2,4},{4,6},{6,7},{7,5},{5,3},{3,1},{1,0},{8,10},{10,12},{12... | collective-permute-start | bytes 2359304 | tf_op jit(solution)/shard_map/ppermute | solution.py:173
  114.7 17.5 %collective-permute-start.11 = (f32[2,32,3072]{2,1,0:T(8,128)S(1)}, f32[2,32,3072]{2,1,0:T(8,128)S(1)}, u32[]{:S(2)}, u32[]{:S(2)}) collective-permute-start(f32[2,32,3072]{2,1,0:T(8,128)S(1)} %collective-permute-done.9), channel_id=1, source_target_pairs={{2,0},{4,2},{6,4},{7,6},{5,7},{3,5},{1,3},{0,1},{10,8},{12,10},{14... | collective-permute-start | bytes 2359304 | tf_op jit(solution)/shard_map/ppermute | solution.py:174
  115.3 31.6 %slice-start.2 = ((s8[12582912]{0:T(1024)(128)(4,1)}), s8[4194304]{0:T(1024)(128)(4,1)S(1)}, s32[]{:S(2)}) async-start(s8[12582912]{0:T(1024)(128)(4,1)} %bitcast.197), calls=%async_computation.5 | async-start | bytes 8388608
  129.4 15.0 %collective-permute-start.12 = (f32[2,32,3072]{2,1,0:T(8,128)S(1)}, f32[2,32,3072]{2,1,0:T(8,128)S(1)}, u32[]{:S(2)}, u32[]{:S(2)}) collective-permute-start(f32[2,32,3072]{2,1,0:T(8,128)S(1)} %collective-permute-done.10), channel_id=1, source_target_pairs={{0,2},{2,4},{4,6},{6,7},{7,5},{5,3},{3,1},{1,0},{8,10},{10,12},{12... | collective-permute-start | bytes 2359304 | tf_op jit(solution)/shard_map/ppermute | solution.py:173
  132.2 14.7 %collective-permute-start.13 = (f32[2,32,3072]{2,1,0:T(8,128)S(1)}, f32[2,32,3072]{2,1,0:T(8,128)S(1)}, u32[]{:S(2)}, u32[]{:S(2)}) collective-permute-start(f32[2,32,3072]{2,1,0:T(8,128)S(1)} %collective-permute-done.11), channel_id=1, source_target_pairs={{2,0},{4,2},{6,4},{7,6},{5,7},{3,5},{1,3},{0,1},{10,8},{12,10},{14... | collective-permute-start | bytes 2359304 | tf_op jit(solution)/shard_map/ppermute | solution.py:174
  163.5 38.6 %copy-start.4 = (f32[128,128]{1,0:T(8,128)S(1)}, f32[128,128]{1,0:T(8,128)}, u32[]{:S(2)}) copy-start(f32[128,128]{1,0:T(8,128)} %fusion.56) | copy-start | bytes 196612
  205.6 35.4 %copy-start.3 = (f32[128,128]{1,0:T(8,128)S(1)}, f32[128,128]{1,0:T(8,128)}, u32[]{:S(2)}) copy-start(f32[128,128]{1,0:T(8,128)} %fusion.58) | copy-start | bytes 196612
  216.4 21.0 %all-to-all-start = ((f32[2,32,2048]{2,0,1:T(2,128)}), f32[2,32,2048]{2,0,1:T(2,128)S(1)}, u32[]{:S(2)}, u32[]{:S(2)}) async-start(f32[2,32,2048]{2,0,1:T(2,128)} %copy.146), calls=%async_computation.1 | async-start | bytes 1048576 | tf_op jit(solution)/shard_map/all_to_all | solution.py:152
  259.9 5.0 %copy-start.1 = (s32[21]{0:T(128)S(1)}, s32[21]{0:T(128)}, u32[]{:S(2)}) copy-start(s32[21]{0:T(128)} %param.27) | copy-start | bytes 256
Sparse Core Ops, SparseCore 0:
  170.5 31.4 reduce-scatter.1
